TPU v7x, 256 devices: a whole 4x4x8 slice. The times are simulated.
256 devices in a mesh: gx: 64 (over z, y, core), gy: 4 (over x).
Axes of the slice: x: 4, y: 4, z: 8, core: 2. Of those that a mesh axis runs over, the one named last changes fastest.
Arguments:
- embeds: bfloat16 [256, 2048, 768], P('gx', 'gy'), may hold values from -6 to 6
- fetch_list: int32 [2, 64, 64], replicated, may hold values from 0 to 16383, as said below
- partners: int32 [2, 64, 64, 2], replicated, may hold values from 0 to 255, as said below
- counts: int32 [256], replicated, may hold values from 512 to 2048
Outputs:
- nearest: float32 [256, 2048], P('gx', 'gy')
Inputs may be any that keep to these rules, and one draw needn't show every extreme that they name: fetch_list[w, h, g] // 64 is a block stored by index g of gx, that is g * 4 <= fetch_list[w, h, g] // 64 < (g + 1) * 4. partners[w, h, g, :] are 2 different blocks stored by index h of gx, none equal to fetch_list[w, h, g] // 64.
All inputs are finite; a program needn't handle non-finite values.
Results may differ from a plain program's by a relative error of at most 0.0003.
Values may be sent and summed in bfloat16 or wider, within the bound.
No kernel may reach another device: no remote copies, remote signals or barrier semaphores. Data moves between devices by JAX's collectives and lax.ppermute only.
A program may use at most 192 MiB of HBM per device.

v0:
```python
import jax
import jax.numpy as jnp
from jax import lax
from jax.sharding import PartitionSpec as P

SLICE = 8


EPS = 1e-06


def normalize(source):
    values = source.astype(jnp.float32)
    return (values * lax.rsqrt(jnp.sum(values * values, axis=-1, keepdims=True) + EPS)).astype(
        jnp.bfloat16
    )


def dense_tiles(arrived, row_valid, chosen, owned_full, col_valid):
    slots, lent_rows, width = arrived.shape
    owned, block, _ = owned_full.shape
    flat_rows = arrived.reshape(slots * lent_rows, width)
    listed = jnp.any(
        chosen[:, :, None] == jnp.arange(owned, dtype=jnp.int32)[None, None, :], axis=1
    )
    listed_pairs = jnp.transpose(listed.reshape(slots, owned // 2, 2), (1, 0, 2))
    column_pairs = owned_full.reshape(owned // 2, 2, block, width)
    valid_pairs = col_valid.reshape(owned // 2, 2, block)

    def advance(best_rows, entries):
        columns, picked, valid_cols = entries
        scores = jnp.einsum("rd,cbd->rcb", flat_rows, columns, preferred_element_type=jnp.float32)
        scores = scores.reshape(slots, lent_rows, 2, block)
        keep = row_valid[:, :, None, None] & picked[:, None, :, None] & valid_cols[None, None, :, :]
        scores = jnp.where(keep, scores, jnp.float32(-1.0))
        return (jnp.maximum(best_rows, jnp.max(scores, axis=(2, 3))), jnp.max(scores, axis=(0, 1)))

    start = jnp.full((slots, lent_rows), -1.0, jnp.float32)
    best_rows, col_parts = lax.scan(advance, start, (column_pairs, listed_pairs, valid_pairs))
    return (best_rows, col_parts.reshape(owned, block))


def on_device(embeds, fetch_list, partners, counts):
    owned, quarter, width = embeds.shape
    slice_rows = SLICE
    pieces = quarter // slice_rows
    my_group = lax.axis_index("gx")
    my_lane = lax.axis_index("gy")
    block = quarter * lax.axis_size("gy")
    first = my_group * owned
    waves = fetch_list.shape[0]
    own_unit = normalize(embeds)
    own_pieces = own_unit.reshape(owned, pieces, slice_rows, width)
    owned_full = lax.all_gather(own_unit, "gy", axis=1, tiled=True)
    positions = jnp.arange(block, dtype=jnp.int32)
    own_counts = lax.dynamic_slice_in_dim(counts, first, owned)
    col_valid = positions[None, :] < own_counts[:, None]
    row_positions = my_lane * quarter + jnp.arange(quarter, dtype=jnp.int32)
    slice_offsets = my_lane * quarter + jnp.arange(slice_rows, dtype=jnp.int32)
    local_ids = jnp.arange(owned, dtype=jnp.int32)
    piece_ids = jnp.arange(pieces, dtype=jnp.int32)
    row_total = jnp.full((owned, quarter), -1.0, jnp.float32)
    col_total = jnp.full((owned, block), -1.0, jnp.float32)
    for wave_index in range(waves):
        tiles = lax.dynamic_index_in_dim(fetch_list[wave_index], my_group, 1, False)
        outgoing_sent_block = tiles // pieces - first
        outgoing_sent_piece = tiles % pieces
        outbound = own_pieces[outgoing_sent_block, outgoing_sent_piece]
        arrived = lax.all_to_all(outbound, "gx", split_axis=0, concat_axis=0, tiled=True)
        incoming = lax.dynamic_index_in_dim(fetch_list[wave_index], my_group, 0, False)
        arrived_counts = counts[incoming // pieces]
        arrived_rows = (incoming % pieces)[:, None] * slice_rows + slice_offsets[None, :]
        row_valid = arrived_rows < arrived_counts[:, None]
        chosen = lax.dynamic_index_in_dim(partners[wave_index], my_group, 0, False) - first
        row_best, col_best = dense_tiles(arrived, row_valid, chosen, owned_full, col_valid)
        returned = lax.all_to_all(row_best, "gx", split_axis=0, concat_axis=0, tiled=True)
        match = (outgoing_sent_block[:, None, None] == local_ids[None, :, None]) & (
            outgoing_sent_piece[:, None, None] == piece_ids[None, None, :]
        )
        placed = jnp.max(
            jnp.where(match[:, :, :, None], returned[:, None, None, :], jnp.float32(-1.0)), axis=0
        )
        row_total = jnp.maximum(row_total, placed.reshape(owned, quarter))
        col_total = jnp.maximum(col_total, col_best)
    col_all = lax.pmax(col_total, "gy")
    col_mine = lax.dynamic_slice_in_dim(col_all, my_lane * quarter, quarter, 1)
    nearest = jnp.maximum(row_total, col_mine)
    mine_valid = row_positions[None, :] < own_counts[:, None]
    return jnp.where(mine_valid, nearest, jnp.float32(-1.0))


def solution(mesh):
    in_specs = (P("gx", "gy", None), P(), P(), P())
    out_specs = P("gx", "gy")
    return jax.shard_map(
        on_device, mesh=mesh, in_specs=in_specs, out_specs=out_specs, check_vma=False
    )
```

profile of v0, /device:TPU:1, one launch (start us, length us, event | category | flops | bytes accessed | tf_op | source)
XLA Modules:
  0.0 224.2 jit_solution(3750707437659595756)
XLA Ops:
  6.5 2.7 %fusion.18 = f32[4,512]{1,0:T(4,128)S(1)} fusion(bf16[4,512,768]{2,1,0:T(8,128)(2,1)} %param.8), kind=kLoop, calls=%fused_computation.36 | loop fusion | flops 4716544 | bytes 3153920 | tf_op jit(solution)/shard_map/reduce_sum | solution.py:14
  9.3 4.1 %fusion.19 = bf16[4,512,768]{2,1,0:T(8,128)(2,1)} fusion(bf16[4,512,768]{2,1,0:T(8,128)(2,1)} %param.8, f32[4,512]{1,0:T(4,128)S(1)} %add_rsqrt_fusion), kind=kLoop, calls=%fused_computation.37 | loop fusion | flops 4718592 | bytes 6299648 | tf_op jit(solution)/shard_map/convert_element_type | solution.py:14
  13.7 2.2 %fusion.48 = bf16[4,64,8,768]{3,2,1,0:T(8,128)(2,1)} fusion(f32[4,512]{1,0:T(4,128)S(1)} %add_rsqrt_fusion, bf16[4,512,768]{2,1,0:T(8,128)(2,1)S(1)} %copy-done.1), kind=kLoop, calls=%fused_computation.135 | loop fusion | flops 4718592 | bytes 6299648 | tf_op jit(solution)/shard_map/reshape | solution.py:53
  16.0 3.5 %gather_fusion.3 = bf16[64,8,768]{2,1,0:T(8,128)(2,1)} fusion(bf16[4,64,8,768]{3,2,1,0:T(8,128)(2,1)} %fusion.48, s32[64]{0:T(128)S(1)} %fusion.42), kind=kCustom, calls=%fused_computation.3 | custom fusion | bytes 1573376 | tf_op jit(solution)/shard_map/gather | solution.py:68
  19.4 13.1 %all-to-all-start.2 = ((bf16[64,8,768]{2,1,0:T(8,128)(2,1)}), bf16[64,8,768]{2,1,0:T(8,128)(2,1)S(1)}, u32[]{:S(2)}, u32[]{:S(2)}) async-start(bf16[64,8,768]{2,1,0:T(8,128)(2,1)} %gather_fusion.3), calls=%async_computation.2 | async-start | bytes 1572864 | tf_op jit(solution)/shard_map/all_to_all | solution.py:69
  32.9 0.8 gather_fusion.2
  33.9 3.7 %gather_fusion.1 = bf16[64,8,768]{2,1,0:T(8,128)(2,1)} fusion(bf16[4,64,8,768]{3,2,1,0:T(8,128)(2,1)} %fusion.48, s32[64]{0:T(128)S(1)} %fusion.43), kind=kCustom, calls=%fused_computation.1 | custom fusion | bytes 1573376 | tf_op jit(solution)/shard_map/gather | solution.py:68
  37.7 0.8 gather_fusion
  39.2 16.4 %all-to-all-done.2 = bf16[64,8,768]{2,1,0:T(8,128)(2,1)S(1)} async-done(((bf16[64,8,768]{2,1,0:T(8,128)(2,1)}), bf16[64,8,768]{2,1,0:T(8,128)(2,1)S(1)}, u32[]{:S(2)}, u32[]{:S(2)}) %all-to-all-start.2) | async-done | bytes 786464 | tf_op jit(solution)/shard_map/all_to_all | solution.py:69
  55.6 5.9 %all-to-all-start = ((bf16[64,8,768]{2,1,0:T(8,128)(2,1)}), bf16[64,8,768]{2,1,0:T(8,128)(2,1)S(1)}, u32[]{:S(2)}, u32[]{:S(2)}) async-start(bf16[64,8,768]{2,1,0:T(8,128)(2,1)} %gather_fusion.1), calls=%async_computation | async-start | bytes 1572864 | tf_op jit(solution)/shard_map/all_to_all | solution.py:69
  61.5 76.8 %all-gather.2.cloned.1.call-done = bf16[4,2048,768]{2,1,0:T(8,128)(2,1)} async-done(((bf16[4,512,768]{2,1,0:T(8,128)(2,1)}), bf16[4,2048,768]{2,1,0:T(8,128)(2,1)}) %all-gather.2.cloned.1.call-update) | async-done | bytes 12582928 | tf_op jit(solution)/shard_map/all_gather | solution.py:54
  138.3 15.5 %while.27 = (s32[]{:T(128)}, f32[64,8]{1,0:T(8,128)}, f32[2,2,2048]{2,1,0:T(2,128)S(1)}, pred[2,64,2]{1,2,0:T(4,128)(4,1)S(1)}, pred[2,2,2048]{2,1,0:T(4,128)(4,...) while((s32[]{:T(128)}, f32[64,8]{1,0:T(8,128)}, ...), condition=%wide.region_11.12_spmd.clone, body=%wide.region_8.11_spmd.clone.sunk | while | flops 3229612544 | bytes 7160887 | solution.py:39
  138.8 6.2 %fusion.52 = (f32[2,2048]{1,0:T(2,128)S(1)}, f32[512]{0:T(512)S(1)}) fusion(pred[2,2048]{1,0:T(4,128)(4,1)S(1)} %dynamic-slice_bitcast_fusion.10, pred[512,2]{0,1:T(4,128)(4,1)S(1)} %broadcast_and_fusion.7, bf16[512,768]{1,0:T(8,128)(2,1)S(1)} %get-tuple-element.389, bf16[2,2,2048,768]{3,2,1,0:T(8,128)(2,1)} %get-tuple-element.388, s32[]{:T(128)S(6)} %copy.19), kind=kOutput, calls=%fused_computation.21.clone.1 | convolution fusion | flops 3229609472 | bytes 7101444 | tf_op jit(solution)/shard_map/while/body/eval_jaxpr/rd,cbd->rcb/dot_general | solution.py:32
  146.2 6.2 %fusion.52 = (f32[2,2048]{1,0:T(2,128)S(1)}, f32[512]{0:T(512)S(1)}) fusion(pred[2,2048]{1,0:T(4,128)(4,1)S(1)} %dynamic-slice_bitcast_fusion.10, pred[512,2]{0,1:T(4,128)(4,1)S(1)} %broadcast_and_fusion.7, bf16[512,768]{1,0:T(8,128)(2,1)S(1)} %get-tuple-element.389, bf16[2,2,2048,768]{3,2,1,0:T(8,128)(2,1)} %get-tuple-element.388, s32[]{:T(128)S(6)} %copy.19), kind=kOutput, calls=%fused_computation.21.clone.1 | convolution fusion | flops 3229609472 | bytes 7101444 | tf_op jit(solution)/shard_map/while/body/eval_jaxpr/rd,cbd->rcb/dot_general | solution.py:32
  152.5 1.4 select_maximum_fusion.5
  153.9 10.9 %all-to-all-start.3 = ((f32[64,1,8]{2,1,0:T(1,128)}), f32[64,1,8]{2,1,0:T(1,128)S(1)}, u32[]{:S(2)}, u32[]{:S(2)}) async-start(f32[64,1,8]{2,1,0:T(1,128)} %bitcast.18), calls=%async_computation.3 | async-start | bytes 65536 | tf_op jit(solution)/shard_map/all_to_all | solution.py:76
  164.8 15.5 %while.26 = (s32[]{:T(128)}, f32[64,8]{1,0:T(8,128)}, f32[2,2,2048]{2,1,0:T(2,128)S(1)}, pred[2,64,2]{1,2,0:T(4,128)(4,1)S(1)}, pred[2,2,2048]{2,1,0:T(4,128)(4,...) while((s32[]{:T(128)}, f32[64,8]{1,0:T(8,128)}, ...), condition=%wide.region_5.6_spmd.clone, body=%wide.region_2.5_spmd.clone.sunk | while | flops 3229612544 | bytes 7160887 | solution.py:39
  165.2 6.2 %fusion.51 = (f32[2,2048]{1,0:T(2,128)S(1)}, f32[512]{0:T(512)S(1)}) fusion(pred[2,2048]{1,0:T(4,128)(4,1)S(1)} %dynamic-slice_bitcast_fusion.8, pred[512,2]{0,1:T(4,128)(4,1)S(1)} %broadcast_and_fusion.6, bf16[512,768]{1,0:T(8,128)(2,1)S(1)} %get-tuple-element.425, bf16[2,2,2048,768]{3,2,1,0:T(8,128)(2,1)} %get-tuple-element.424, s32[]{:T(128)S(6)} %copy.28), kind=kOutput, calls=%fused_computation.7.clone.1 | convolution fusion | flops 3229609472 | bytes 7101444 | tf_op jit(solution)/shard_map/while/body/eval_jaxpr/rd,cbd->rcb/dot_general | solution.py:32
  172.6 6.2 %fusion.51 = (f32[2,2048]{1,0:T(2,128)S(1)}, f32[512]{0:T(512)S(1)}) fusion(pred[2,2048]{1,0:T(4,128)(4,1)S(1)} %dynamic-slice_bitcast_fusion.8, pred[512,2]{0,1:T(4,128)(4,1)S(1)} %broadcast_and_fusion.6, bf16[512,768]{1,0:T(8,128)(2,1)S(1)} %get-tuple-element.425, bf16[2,2,2048,768]{3,2,1,0:T(8,128)(2,1)} %get-tuple-element.424, s32[]{:T(128)S(6)} %copy.28), kind=kOutput, calls=%fused_computation.7.clone.1 | convolution fusion | flops 3229609472 | bytes 7101444 | tf_op jit(solution)/shard_map/while/body/eval_jaxpr/rd,cbd->rcb/dot_general | solution.py:32
  178.9 1.4 select_maximum_fusion.4
  180.4 12.3 %pmax.7 = f32[4,2048]{1,0:T(4,128)S(1)} all-reduce(f32[4,2048]{1,0:T(4,128)S(1)} %max.26), channel_id=1, replica_groups=mesh['gx'=64,'gy'=4] {'gy'}, use_global_device_ids=true, to_apply=%region_13.14 | all-reduce | flops 8192 | bytes 65536 | tf_op jit(solution)/shard_map/pmax | solution.py:85
  192.7 14.1 %all-to-all-start.1 = ((f32[64,1,8]{2,1,0:T(1,128)}), f32[64,1,8]{2,1,0:T(1,128)S(1)}, u32[]{:S(2)}, u32[]{:S(2)}) async-start(f32[64,1,8]{2,1,0:T(1,128)} %bitcast.9), calls=%async_computation.1 | async-start | bytes 65536 | tf_op jit(solution)/shard_map/all_to_all | solution.py:76
  207.0 9.2 %all-to-all-done.1 = f32[64,1,8]{2,1,0:T(1,128)S(1)} async-done(((f32[64,1,8]{2,1,0:T(1,128)}), f32[64,1,8]{2,1,0:T(1,128)S(1)}, u32[]{:S(2)}, u32[]{:S(2)}) %all-to-all-start.1) | async-done | bytes 2080 | tf_op jit(solution)/shard_map/all_to_all | solution.py:76
  216.6 0.7 maximum_select_fusion
  (90 shorter events, 5.4 us)
Async XLA Ops:
  6.5 7.2 %copy-start.1 = (bf16[4,512,768]{2,1,0:T(8,128)(2,1)S(1)}, bf16[4,512,768]{2,1,0:T(8,128)(2,1)}, u32[]{:S(2)}) copy-start(bf16[4,512,768]{2,1,0:T(8,128)(2,1)} %param.8) | copy-start | bytes 9437188
  6.5 6.9 %copy-start.3 = (s32[2,64,64]{2,1,0:T(8,128)S(1)}, s32[2,64,64]{2,1,0:T(8,128)}, u32[]{:S(2)}) copy-start(s32[2,64,64]{2,1,0:T(8,128)} %param.9) | copy-start | bytes 98308
  6.5 131.8 %all-gather.2.cloned.1.call-start = ((), (), s32[]{:S(2)}) async-start(), calls=%async_computation.4 | async-start | bytes 15728640 | tf_op jit(solution)/shard_map/all_gather | solution.py:54
  13.4 19.2 %copy-start.2 = (s32[2,64,64,2]{2,3,1,0:T(2,128)S(1)}, s32[2,64,64,2]{2,3,1,0:T(2,128)}, u32[]{:S(2)}) copy-start(s32[2,64,64,2]{2,3,1,0:T(2,128)} %param.10) | copy-start | bytes 196612
  13.4 19.2 %copy-start = (s32[256]{0:T(256)S(1)}, s32[256]{0:T(256)}, u32[]{:S(2)}) copy-start(s32[256]{0:T(256)} %param.11) | copy-start | bytes 3076
  19.4 36.2 %all-to-all-start.2 = ((bf16[64,8,768]{2,1,0:T(8,128)(2,1)}), bf16[64,8,768]{2,1,0:T(8,128)(2,1)S(1)}, u32[]{:S(2)}, u32[]{:S(2)}) async-start(bf16[64,8,768]{2,1,0:T(8,128)(2,1)} %gather_fusion.3), calls=%async_computation.2 | async-start | bytes 1572864 | tf_op jit(solution)/shard_map/all_to_all | solution.py:69
  55.6 98.3 %all-to-all-start = ((bf16[64,8,768]{2,1,0:T(8,128)(2,1)}), bf16[64,8,768]{2,1,0:T(8,128)(2,1)S(1)}, u32[]{:S(2)}, u32[]{:S(2)}) async-start(bf16[64,8,768]{2,1,0:T(8,128)(2,1)} %gather_fusion.1), calls=%async_computation | async-start | bytes 1572864 | tf_op jit(solution)/shard_map/all_to_all | solution.py:69
  153.9 38.8 %all-to-all-start.3 = ((f32[64,1,8]{2,1,0:T(1,128)}), f32[64,1,8]{2,1,0:T(1,128)S(1)}, u32[]{:S(2)}, u32[]{:S(2)}) async-start(f32[64,1,8]{2,1,0:T(1,128)} %bitcast.18), calls=%async_computation.3 | async-start | bytes 65536 | tf_op jit(solution)/shard_map/all_to_all | solution.py:76
  192.7 23.5 %all-to-all-start.1 = ((f32[64,1,8]{2,1,0:T(1,128)}), f32[64,1,8]{2,1,0:T(1,128)S(1)}, u32[]{:S(2)}, u32[]{:S(2)}) async-start(f32[64,1,8]{2,1,0:T(1,128)} %bitcast.9), calls=%async_computation.1 | async-start | bytes 65536 | tf_op jit(solution)/shard_map/all_to_all | solution.py:76
Sparse Core Ops, SparseCore 0:
  13.6 124.6 all-gather.1
where the time goes:
time: 225 us; the launch traced here: 224 us
  waiting for transfers between devices  102 us (45%)
  starting transfers between devices  44 us (20%)
  matrix products  24.8 us (11%)
  other arithmetic  15.5 us (7%)
  between operations  13.7 us (6%)
  blocking collectives  12.3 us (5%)
  local copies, waits for them, and re-layouts  11.2 us (5%)
    all_gather x1, waiting for transfers between devices, on_device(): owned_full = lax.all_gather(own_unit, 'gy', axis=1, tiled=True)  76.8 us
    all_to_all x2, starting transfers between devices, on_device(): lax.all_to_all(row_best, 'gx', split_axis=0, concat_axis=0, tiled=True)  24.9 us
    dot_general x4, matrix products, advance(): jnp.einsum('rd,cbd->rcb', flat_rows, columns, preferred_element_type=jnp....  24.8 us
    all_to_all x2, starting transfers between devices, on_device(): lax.all_to_all(outbound, 'gx', split_axis=0, concat_axis=0, tiled=True)  19.1 us
    all_to_all x2, waiting for transfers between devices, on_device(): lax.all_to_all(outbound, 'gx', split_axis=0, concat_axis=0, tiled=True)  16.4 us
    pmax x1, blocking collectives, on_device(): col_all = lax.pmax(col_total, 'gy')  12.3 us
    all_to_all x2, waiting for transfers between devices, on_device(): lax.all_to_all(row_best, 'gx', split_axis=0, concat_axis=0, tiled=True)  9.17 us
    gather x2, local copies, waits for them, and re-layouts, on_device(): outbound = own_pieces[outgoing_sent_block, outgoing_sent_piece]  7.19 us
  transfers between devices with their start and end apart: 5, of which 3 were waited for; matrix products, arithmetic and copies ran while one was open for 19% of the time, Pallas kernels for 0%

commit v1 on v0

v1 whole, which is shorter than its diff:
```python
import jax
import jax.numpy as jnp
from jax import lax
from jax.sharding import PartitionSpec as P

SLICE = 8


EPS = 1e-06


def normalize(source):
    values = source.astype(jnp.float32)
    return (values * lax.rsqrt(jnp.sum(values * values, axis=-1, keepdims=True) + EPS)).astype(
        jnp.bfloat16
    )


def lent_scores(lent, row_valid, listed, own_unit, col_valid):
    slots, lanes, lent_rows, width = lent.shape
    owned, quarter, _ = own_unit.shape
    flat_rows = lent.reshape(slots * lanes * lent_rows, width)
    scores = jnp.einsum("rd,kcd->rkc", flat_rows, own_unit, preferred_element_type=jnp.float32)
    scores = scores.reshape(slots, lanes, lent_rows, owned, quarter)
    keep = (
        row_valid[:, :, :, None, None]
        & listed[:, None, None, :, None]
        & col_valid[None, None, None, :, :]
    )
    scores = jnp.where(keep, scores, jnp.float32(-1.0))
    return jnp.max(scores, axis=(3, 4)), jnp.max(scores, axis=(0, 1, 2))


def on_device(embeds, fetch_list, partners, counts):
    owned, quarter, width = embeds.shape
    slice_rows = SLICE
    pieces = quarter // slice_rows
    my_group = lax.axis_index("gx")
    my_lane = lax.axis_index("gy")
    n_gy = lax.axis_size("gy")
    first = my_group * owned
    waves = fetch_list.shape[0]
    own_unit = normalize(embeds)
    own_pieces = own_unit.reshape(owned, pieces, slice_rows, width)
    own_counts = lax.dynamic_slice_in_dim(counts, first, owned)
    col_positions = my_lane * quarter + jnp.arange(quarter, dtype=jnp.int32)
    col_valid = col_positions[None, :] < own_counts[:, None]
    lane_rows = (
        jnp.arange(n_gy, dtype=jnp.int32)[:, None] * quarter
        + jnp.arange(slice_rows, dtype=jnp.int32)[None, :]
    )
    local_ids = jnp.arange(owned, dtype=jnp.int32)
    piece_ids = jnp.arange(pieces, dtype=jnp.int32)
    col_total = jnp.full((owned, quarter), -1.0, jnp.float32)
    row_parts = []
    sent_blocks = []
    sent_pieces = []
    for wave_index in range(waves):
        tiles = lax.dynamic_index_in_dim(fetch_list[wave_index], my_group, 1, False)
        outgoing_sent_block = tiles // pieces - first
        outgoing_sent_piece = tiles % pieces
        sent_blocks.append(outgoing_sent_block)
        sent_pieces.append(outgoing_sent_piece)
        outbound = own_pieces[outgoing_sent_block, outgoing_sent_piece]
        arrived = lax.all_to_all(outbound, "gx", split_axis=0, concat_axis=0, tiled=True)
        lent = lax.all_gather(arrived, "gy", axis=1, tiled=False)
        incoming = lax.dynamic_index_in_dim(fetch_list[wave_index], my_group, 0, False)
        arrived_counts = counts[incoming // pieces]
        arrived_rows = (incoming % pieces)[:, None, None] * slice_rows + lane_rows[None, :, :]
        row_valid = arrived_rows < arrived_counts[:, None, None]
        chosen = lax.dynamic_index_in_dim(partners[wave_index], my_group, 0, False) - first
        listed = jnp.any(chosen[:, :, None] == local_ids[None, None, :], axis=1)
        row_best, col_best = lent_scores(lent, row_valid, listed, own_unit, col_valid)
        row_parts.append(row_best)
        col_total = jnp.maximum(col_total, col_best)
    row_all = jnp.stack(row_parts, axis=0)
    groups = row_all.shape[1]
    outgoing = jnp.transpose(row_all, (1, 2, 0, 3)).reshape(groups * n_gy, waves, slice_rows)
    returned = lax.all_to_all(outgoing, ("gx", "gy"), split_axis=0, concat_axis=0, tiled=True)
    returned = jnp.max(returned.reshape(groups, n_gy, waves, slice_rows), axis=1)
    row_total = jnp.full((owned, pieces, slice_rows), -1.0, jnp.float32)
    for wave_index in range(waves):
        match = (sent_blocks[wave_index][:, None, None] == local_ids[None, :, None]) & (
            sent_pieces[wave_index][:, None, None] == piece_ids[None, None, :]
        )
        placed = jnp.max(
            jnp.where(
                match[:, :, :, None], returned[:, wave_index][:, None, None, :], jnp.float32(-1.0)
            ),
            axis=0,
        )
        row_total = jnp.maximum(row_total, placed)
    nearest = jnp.maximum(row_total.reshape(owned, quarter), col_total)
    mine_valid = col_positions[None, :] < own_counts[:, None]
    return jnp.where(mine_valid, nearest, jnp.float32(-1.0))


def solution(mesh):
    in_specs = (P("gx", "gy", None), P(), P(), P())
    out_specs = P("gx", "gy")
    return jax.shard_map(
        on_device, mesh=mesh, in_specs=in_specs, out_specs=out_specs, check_vma=False
    )
```

time: 225 us -> 189 us (0.84)
  waiting for transfers between devices: 102 us -> 69 us
  starting transfers between devices: 44 us -> 18.4 us
  blocking collectives: 12.3 us -> 36.2 us
  other arithmetic: 15.5 us -> 12.4 us
    all_gather x1 -> x2, waiting for transfers between devices: 76.8 us -> 33.7 us  [on_device(): lent = lax.all_gather(arrived, 'gy', axis=1, tiled=False)]
    all_to_all x0 -> x1, blocking collectives: none -> 36.2 us  [on_device(): lax.all_to_all(outbound, 'gx', split_axis=0, concat_axis=0, tiled=True)]
    all_to_all x2 -> x1, starting transfers between devices: 19.1 us -> 6.07 us  [on_device(): lax.all_to_all(outbound, 'gx', split_axis=0, concat_axis=0, tiled=True)]
    all_to_all x2 -> x1, starting transfers between devices: 24.9 us -> 12.3 us  [on_device(): lax.all_to_all(outgoing, ('gx', 'gy'), split_axis=0, concat_axis=0, tiled...]
    pmax x1 -> x0, blocking collectives: 12.3 us -> none  [on_device(): col_all = lax.pmax(col_total, 'gy')]
    all_to_all x2 -> x1, waiting for transfers between devices: 9.17 us -> 14.4 us  [on_device(): lax.all_to_all(outgoing, ('gx', 'gy'), split_axis=0, concat_axis=0, tiled...]
    all_to_all x2 -> x1, waiting for transfers between devices: 16.4 us -> 20.9 us  [on_device(): lax.all_to_all(outbound, 'gx', split_axis=0, concat_axis=0, tiled=True)]
    convert_element_type x1 -> x0, other arithmetic: 4.14 us -> none  [normalize(): (values * lax.rsqrt(jnp.sum(values * values, axis=-1, keepdims=True) + EP...]
  transfers between devices with their start and end apart: 5 -> 4, of which waited for: 3 -> 4; matrix products, arithmetic and copies ran while one was open for 19% -> 12% of each run, Pallas kernels for 0% -> 0%
where the time goes in v1:
time: 189 us; the launch traced here: 188 us
  waiting for transfers between devices  69 us (37%)
  blocking collectives  36.2 us (19%)
  matrix products  26.9 us (14%)
  starting transfers between devices  18.4 us (10%)
  between operations  13.6 us (7%)
  other arithmetic  12.4 us (7%)
  local copies, waits for them, and re-layouts  11.4 us (6%)
    all_to_all x1, blocking collectives, on_device(): lax.all_to_all(outbound, 'gx', split_axis=0, concat_axis=0, tiled=True)  36.2 us
    all_gather x2, waiting for transfers between devices, on_device(): lent = lax.all_gather(arrived, 'gy', axis=1, tiled=False)  33.7 us
    dot_general x2, matrix products, lent_scores(): jnp.einsum('rd,kcd->rkc', flat_rows, own_unit, preferred_element_type=jnp...  26.9 us
    all_to_all x1, waiting for transfers between devices, on_device(): lax.all_to_all(outbound, 'gx', split_axis=0, concat_axis=0, tiled=True)  20.9 us
    all_to_all x1, waiting for transfers between devices, on_device(): lax.all_to_all(outgoing, ('gx', 'gy'), split_axis=0, concat_axis=0, tiled...  14.4 us
    all_to_all x1, starting transfers between devices, on_device(): lax.all_to_all(outgoing, ('gx', 'gy'), split_axis=0, concat_axis=0, tiled...  12.3 us
    gather x2, local copies, waits for them, and re-layouts, on_device(): outbound = own_pieces[outgoing_sent_block, outgoing_sent_piece]  6.93 us
    all_to_all x1, starting transfers between devices, on_device(): lax.all_to_all(outbound, 'gx', split_axis=0, concat_axis=0, tiled=True)  6.07 us
  transfers between devices with their start and end apart: 4, of which 4 were waited for; matrix products, arithmetic and copies ran while one was open for 12% of the time, Pallas kernels for 0%

profile of v1, /device:TPU:1, one launch (start us, length us, event | category | flops | bytes accessed | tf_op | source)
XLA Modules:
  0.0 188.0 jit_solution(5584732037155521731)
XLA Ops:
  6.5 0.9 fusion.43
  7.5 2.6 %fusion.4 = f32[4,512]{1,0:T(4,128)S(1)} fusion(bf16[4,512,768]{2,1,0:T(8,128)(2,1)} %param.4), kind=kLoop, calls=%fused_computation.12 | loop fusion | flops 4716544 | bytes 3153920 | tf_op jit(solution)/shard_map/reduce_sum | solution.py:14
  10.1 2.2 %fusion.14 = bf16[4,64,8,768]{3,2,1,0:T(8,128)(2,1)} fusion(f32[4,512]{1,0:T(4,128)S(1)} %add_rsqrt_fusion, bf16[4,512,768]{2,1,0:T(8,128)(2,1)S(1)} %copy-done.1), kind=kLoop, calls=%fused_computation.20 | loop fusion | flops 4718592 | bytes 6299648 | tf_op jit(solution)/shard_map/reshape | solution.py:44
  12.6 3.5 %gather_fusion.3 = bf16[64,8,768]{2,1,0:T(8,128)(2,1)} fusion(bf16[4,64,8,768]{3,2,1,0:T(8,128)(2,1)} %fusion.14, s32[64]{0:T(128)S(1)} %fusion.37), kind=kCustom, calls=%fused_computation.3 | custom fusion | bytes 1573376 | tf_op jit(solution)/shard_map/gather | solution.py:64
  16.0 36.2 %all_to_all.15 = bf16[64,8,768]{2,1,0:T(8,128)(2,1)} all-to-all(bf16[64,8,768]{2,1,0:T(8,128)(2,1)} %gather_fusion.3), channel_id=1, replica_groups=mesh['gx'=64,'gy'=4] {'gx'}, dimensions={0} | all-to-all | bytes 1572864 | tf_op jit(solution)/shard_map/all_to_all | solution.py:65
  52.5 3.5 %gather_fusion.1 = bf16[64,8,768]{2,1,0:T(8,128)(2,1)} fusion(bf16[4,64,8,768]{3,2,1,0:T(8,128)(2,1)} %fusion.14, s32[64]{0:T(128)S(1)} %fusion.38), kind=kCustom, calls=%fused_computation.1 | custom fusion | bytes 1573376 | tf_op jit(solution)/shard_map/gather | solution.py:64
  56.0 6.1 %all-to-all-start = ((bf16[64,8,768]{2,1,0:T(8,128)(2,1)}), bf16[64,8,768]{2,1,0:T(8,128)(2,1)}, u32[]{:S(2)}, u32[]{:S(2)}) async-start(bf16[64,8,768]{2,1,0:T(8,128)(2,1)} %gather_fusion.1), calls=%async_computation | async-start | bytes 1572864 | tf_op jit(solution)/shard_map/all_to_all | solution.py:65
  62.4 0.8 gather_fusion.2
  63.2 0.8 gather_fusion
  64.1 20.9 %all-to-all-done = bf16[64,8,768]{2,1,0:T(8,128)(2,1)} async-done(((bf16[64,8,768]{2,1,0:T(8,128)(2,1)}), bf16[64,8,768]{2,1,0:T(8,128)(2,1)}, u32[]{:S(2)}, u32[]{:S(2)}) %all-to-all-start) | async-done | bytes 786464 | tf_op jit(solution)/shard_map/all_to_all | solution.py:65
  85.2 0.7 broadcast_compare_fusion
  86.1 0.7 iota_compare_fusion.3
  86.7 0.7 broadcast_and_fusion.2
  88.0 0.8 broadcast_and_fusion
  88.9 2.0 %all-gather.7.cloned.1.call-done = bf16[64,32,768]{2,1,0:T(8,128)(2,1)} async-done(((bf16[64,8,768]{2,1,0:T(8,128)(2,1)}), bf16[64,32,768]{2,1,0:T(8,128)(2,1)}) %all-gather.7.cloned.1.call-update) | async-done | bytes 3145744 | tf_op jit(solution)/shard_map/all_gather | solution.py:66
  90.9 12.3 %fusion.6 = f32[64,4,8,4,512]{4,2,3,1,0:T(8,128)} fusion(bf16[64,32,768]{2,1,0:T(8,128)(2,1)} %all-gather.7.cloned.1.call-done, bf16[4,512,768]{2,1,0:T(8,128)(2,1)S(1)} %copy-done.1, f32[4,512]{1,0:T(4,128)S(1)} %add_rsqrt_fusion), kind=kOutput, calls=%fused_computation.14 | convolution fusion | flops 6447169536 | bytes 23076864 | tf_op jit(solution)/shard_map/rd,kcd->rkc/dot_general | solution.py:23
  103.2 31.7 %all-gather.5.cloned.1.call-done = bf16[64,32,768]{2,1,0:T(8,128)(2,1)} async-done(((bf16[64,8,768]{2,1,0:T(8,128)(2,1)}), bf16[64,32,768]{2,1,0:T(8,128)(2,1)}) %all-gather.5.cloned.1.call-update) | async-done | bytes 3145744 | tf_op jit(solution)/shard_map/all_gather | solution.py:66
  134.9 14.6 %fusion = (f32[4,512]{1,0:T(4,128)}, f32[64,4,8]{2,1,0:T(4,128)S(1)}, f32[64,4,8]{2,1,0:T(4,128)S(1)}, f32[4,512]{1,0:T(4,128)}) fusion(pred[4,512]{1,0:T(4,128)(4,1)} %broadcast_compare_fusion, pred[64,4,8,4]{2,3,1,0:T(4,128)(4,1)S(1)} %broadcast_and_fusion.1, f32[64,4,8,4,512]{4,2,3,1,0:T(8,128)} %fusion.6, pred[64,4,8,4]{2,3,1,0:T(4,128)(4,1)} %broadcast_and_fusion, ...), kind=kOutput, calls=%fused_computation.6 | convolution fusion | flops 6480715776 | bytes 23128064 | tf_op jit(solution)/shard_map/rd,kcd->rkc/dot_general | solution.py:23
  149.7 0.8 copy.21
  150.6 12.3 %all-to-all-start.2 = ((f32[256,2,8]{2,1,0:T(2,128)}), f32[256,2,8]{2,1,0:T(2,128)S(1)}, u32[]{:S(2)}, u32[]{:S(2)}) async-start(f32[256,2,8]{2,1,0:T(2,128)} %bitcast.23), calls=%async_computation.2 | async-start | bytes 524288 | tf_op jit(solution)/shard_map/all_to_all | solution.py:79
  162.8 0.8 broadcast_and_fusion.3
  163.7 14.4 %all-to-all-done.2 = f32[256,2,8]{2,1,0:T(2,128)S(1)} async-done(((f32[256,2,8]{2,1,0:T(2,128)}), f32[256,2,8]{2,1,0:T(2,128)S(1)}, u32[]{:S(2)}, u32[]{:S(2)}) %all-to-all-start.2) | async-done | bytes 16416 | tf_op jit(solution)/shard_map/all_to_all | solution.py:79
  178.3 1.0 select_reduce_fusion
  179.8 1.4 maximum_select_fusion
  (48 shorter events, 2.6 us)
Async XLA Ops:
  6.5 3.6 %copy-start.1 = (bf16[4,512,768]{2,1,0:T(8,128)(2,1)S(1)}, bf16[4,512,768]{2,1,0:T(8,128)(2,1)}, u32[]{:S(2)}) copy-start(bf16[4,512,768]{2,1,0:T(8,128)(2,1)} %param.4) | copy-start | bytes 9437188
  6.5 84.3 %all-gather.7.cloned.1.call-start = ((), (), s32[]{:S(2)}) async-start(), calls=%async_computation.4 | async-start | bytes 3932160 | tf_op jit(solution)/shard_map/all_gather | solution.py:66
  12.4 49.8 %copy-start.2 = (s32[2,64,64,2]{2,3,1,0:T(2,128)S(1)}, s32[2,64,64,2]{2,3,1,0:T(2,128)}, u32[]{:S(2)}) copy-start(s32[2,64,64,2]{2,3,1,0:T(2,128)} %param.6) | copy-start | bytes 196612
  12.4 49.9 %copy-start = (s32[256]{0:T(256)S(1)}, s32[256]{0:T(256)}, u32[]{:S(2)}) copy-start(s32[256]{0:T(256)} %param.7) | copy-start | bytes 3076
  56.0 29.0 %all-to-all-start = ((bf16[64,8,768]{2,1,0:T(8,128)(2,1)}), bf16[64,8,768]{2,1,0:T(8,128)(2,1)}, u32[]{:S(2)}, u32[]{:S(2)}) async-start(bf16[64,8,768]{2,1,0:T(8,128)(2,1)} %gather_fusion.1), calls=%async_computation | async-start | bytes 1572864 | tf_op jit(solution)/shard_map/all_to_all | solution.py:65
  62.1 72.9 %all-gather.5.cloned.1.call-start = ((), (), s32[]{:S(2)}) async-start(), calls=%async_computation.3 | async-start | bytes 3932160 | tf_op jit(solution)/shard_map/all_gather | solution.py:66
  62.4 40.8 %copy-start.4 = (s32[4]{0:T(128)}, s32[4]{0:T(128)S(1)}, u32[]{:S(2)}) copy-start(s32[4]{0:T(128)S(1)} %dynamic_slice.24) | copy-start | bytes 52
  85.1 0.8 copy-start.3
  150.6 27.5 %all-to-all-start.2 = ((f32[256,2,8]{2,1,0:T(2,128)}), f32[256,2,8]{2,1,0:T(2,128)S(1)}, u32[]{:S(2)}, u32[]{:S(2)}) async-start(f32[256,2,8]{2,1,0:T(2,128)} %bitcast.23), calls=%async_computation.2 | async-start | bytes 524288 | tf_op jit(solution)/shard_map/all_to_all | solution.py:79
Sparse Core Ops, SparseCore 0:
  52.4 38.3 all-gather.6
  92.7 42.2 all-gather.4

commit v2 on v1

v2 whole, which is shorter than its diff:
```python
import jax
import jax.numpy as jnp
from jax import lax
from jax.experimental import pallas as pl
from jax.experimental.pallas import tpu as pltpu
from jax.sharding import PartitionSpec as P

SLICE = 8


EPS = 1e-06


def normalize(source):
    values = source.astype(jnp.float32)
    return (values * lax.rsqrt(jnp.sum(values * values, axis=-1, keepdims=True) + EPS)).astype(
        jnp.bfloat16
    )


def _score_kernel(rowmask_ref, colvalid_ref, lhs_ref, rhs_ref, rowmax_ref, colmax_ref):
    step = pl.program_id(0)
    scores = lax.dot_general(
        lhs_ref[...], rhs_ref[...], (((1,), (1,)), ((), ())), preferred_element_type=jnp.float32
    )
    keep = (rowmask_ref[0] > 0) & (colvalid_ref[0] > 0)
    scores = jnp.where(keep, scores, jnp.float32(-1.0))
    row_best = jnp.max(scores, axis=1, keepdims=True)
    colmax_ref[0] = jnp.max(scores, axis=0, keepdims=True)

    @pl.when(step == 0)
    def _():
        rowmax_ref[...] = jnp.broadcast_to(row_best, rowmax_ref.shape)

    @pl.when(step > 0)
    def _():
        rowmax_ref[...] = jnp.maximum(rowmax_ref[...], row_best)


def lent_scores(lent, row_valid, listed, columns, col_valid):
    slots, lent_rows, width = lent.shape
    owned, quarter, _ = columns.shape
    n_rows = slots * lent_rows
    tiles = owned
    flat_rows = lent.reshape(n_rows, width)
    flat_cols = columns.reshape(tiles * quarter, width)
    rowmask = (row_valid[None, :, :] & jnp.transpose(listed)[:, :, None]).astype(jnp.int32)
    rowmask = rowmask.reshape(owned, n_rows, 1)
    colmask = col_valid.astype(jnp.int32).reshape(tiles, 1, quarter)
    rowmax, colmax = pl.pallas_call(
        _score_kernel,
        out_shape=(
            jax.ShapeDtypeStruct((n_rows, 128), jnp.float32),
            jax.ShapeDtypeStruct((tiles, 1, quarter), jnp.float32),
        ),
        grid=(tiles,),
        in_specs=[
            pl.BlockSpec((1, n_rows, 1), lambda j: (j, 0, 0)),
            pl.BlockSpec((1, 1, quarter), lambda j: (j, 0, 0)),
            pl.BlockSpec((n_rows, width), lambda j: (0, 0)),
            pl.BlockSpec((quarter, width), lambda j: (j, 0)),
        ],
        out_specs=[
            pl.BlockSpec((n_rows, 128), lambda j: (0, 0)),
            pl.BlockSpec((1, 1, quarter), lambda j: (j, 0, 0)),
        ],
        compiler_params=pltpu.CompilerParams(dimension_semantics=("arbitrary",)),
        cost_estimate=pl.CostEstimate(
            flops=2 * n_rows * tiles * quarter * width,
            transcendentals=0,
            bytes_accessed=2 * (n_rows + tiles * quarter) * width,
        ),
    )(rowmask, colmask, flat_rows, flat_cols)
    return rowmax[:, 0].reshape(slots, lent_rows), colmax.reshape(owned, quarter)


def on_device(embeds, fetch_list, partners, counts):
    owned, quarter, width = embeds.shape
    slice_rows = SLICE
    pieces = quarter // slice_rows
    my_group = lax.axis_index("gx")
    my_lane = lax.axis_index("gy")
    n_gy = lax.axis_size("gy")
    first = my_group * owned
    waves = fetch_list.shape[0]
    pair_p = [(lane, lane ^ 1) for lane in range(n_gy)]
    pair_r = [(lane, n_gy - 1 - lane) for lane in range(n_gy)]
    lane_p = jnp.bitwise_xor(my_lane, 1)
    lane_r = n_gy - 1 - my_lane
    own_unit = normalize(embeds)
    other_unit = lax.ppermute(own_unit, "gy", pair_p)
    own_pieces = own_unit.reshape(owned, pieces, slice_rows, width)
    own_counts = lax.dynamic_slice_in_dim(counts, first, owned)
    positions = jnp.arange(quarter, dtype=jnp.int32)
    col_sources = []
    for lane, unit in ((my_lane, own_unit), (lane_p, other_unit)):
        col_valid = (lane * quarter + positions)[None, :] < own_counts[:, None]
        col_sources.append((unit, col_valid))
    slice_offsets = jnp.arange(slice_rows, dtype=jnp.int32)
    local_ids = jnp.arange(owned, dtype=jnp.int32)
    piece_ids = jnp.arange(pieces, dtype=jnp.int32)
    col_part = [jnp.full((owned, quarter), -1.0, jnp.float32) for _ in col_sources]
    row_mine_parts = []
    row_other_parts = []
    sent_blocks = []
    sent_pieces = []
    for wave_index in range(waves):
        tiles = lax.dynamic_index_in_dim(fetch_list[wave_index], my_group, 1, False)
        outgoing_sent_block = tiles // pieces - first
        outgoing_sent_piece = tiles % pieces
        sent_blocks.append(outgoing_sent_block)
        sent_pieces.append(outgoing_sent_piece)
        outbound = own_pieces[outgoing_sent_block, outgoing_sent_piece]
        arrived = lax.all_to_all(outbound, "gx", split_axis=0, concat_axis=0, tiled=True)
        arrived_other = lax.ppermute(arrived, "gy", pair_r)
        incoming = lax.dynamic_index_in_dim(fetch_list[wave_index], my_group, 0, False)
        arrived_counts = counts[incoming // pieces]
        chosen = lax.dynamic_index_in_dim(partners[wave_index], my_group, 0, False) - first
        listed = jnp.any(chosen[:, :, None] == local_ids[None, None, :], axis=1)
        piece_rows = (incoming % pieces)[:, None] * slice_rows + slice_offsets[None, :]
        for lane, rows_in, parts in (
            (my_lane, arrived, row_mine_parts),
            (lane_r, arrived_other, row_other_parts),
        ):
            row_valid = (lane * quarter + piece_rows) < arrived_counts[:, None]
            row_best = jnp.full(row_valid.shape, -1.0, jnp.float32)
            for source, (unit, col_valid) in enumerate(col_sources):
                rows_max, col_best = lent_scores(rows_in, row_valid, listed, unit, col_valid)
                row_best = jnp.maximum(row_best, rows_max)
                col_part[source] = jnp.maximum(col_part[source], col_best)
            parts.append(row_best)
    col_back = lax.ppermute(col_part[1], "gy", pair_p)
    col_total = jnp.maximum(col_part[0], col_back)
    row_other = jnp.stack(row_other_parts, axis=0)
    row_back = lax.ppermute(row_other, "gy", pair_r)
    row_mine = jnp.maximum(jnp.stack(row_mine_parts, axis=0), row_back)
    returned = lax.all_to_all(row_mine, "gx", split_axis=1, concat_axis=1, tiled=True)
    row_total = jnp.full((owned, pieces, slice_rows), -1.0, jnp.float32)
    for wave_index in range(waves):
        match = (sent_blocks[wave_index][:, None, None] == local_ids[None, :, None]) & (
            sent_pieces[wave_index][:, None, None] == piece_ids[None, None, :]
        )
        placed = jnp.max(
            jnp.where(
                match[:, :, :, None], returned[wave_index][:, None, None, :], jnp.float32(-1.0)
            ),
            axis=0,
        )
        row_total = jnp.maximum(row_total, placed)
    nearest = jnp.maximum(row_total.reshape(owned, quarter), col_total)
    mine_valid = (my_lane * quarter + positions)[None, :] < own_counts[:, None]
    return jnp.where(mine_valid, nearest, jnp.float32(-1.0))


def solution(mesh):
    in_specs = (P("gx", "gy", None), P(), P(), P())
    out_specs = P("gx", "gy")
    return jax.shard_map(
        on_device, mesh=mesh, in_specs=in_specs, out_specs=out_specs, check_vma=False
    )
```

time: 189 us -> 154 us (0.81)
  Pallas kernels: 0 us -> 45.3 us
  blocking collectives: 36.2 us -> 0 us
  matrix products: 26.9 us -> 0 us
  waiting for transfers between devices: 69 us -> 42.2 us
  starting transfers between devices: 18.4 us -> 34.5 us
  between operations: 13.6 us -> 0.55 us
  local copies, waits for them, and re-layouts: 11.4 us -> 14.9 us
  other arithmetic: 12.4 us -> 15.1 us
    pallas_call x0 -> x8, Pallas kernels: none -> 45.3 us  [lent_scores(): pl.pallas_call(_score_kernel, out_shape=(jax.ShapeDtypeStruct((n_rows, 12...]
    all_to_all x1 -> x0, blocking collectives: 36.2 us -> none  [on_device(): lax.all_to_all(outbound, 'gx', split_axis=0, concat_axis=0, tiled=True)]
    all_gather x2 -> x0, waiting for transfers between devices: 33.7 us -> none  [on_device(): lent = lax.all_gather(arrived, 'gy', axis=1, tiled=False)]
    dot_general x2 -> x0, matrix products: 26.9 us -> none  [lent_scores(): jnp.einsum('rd,kcd->rkc', flat_rows, own_unit, preferred_element_type=jnp...]
    all_to_all x1 -> x2, starting transfers between devices: 6.07 us -> 19.2 us  [on_device(): lax.all_to_all(outbound, 'gx', split_axis=0, concat_axis=0, tiled=True)]
    all_to_all x1 -> x2, waiting for transfers between devices: 20.9 us -> 30.3 us  [on_device(): lax.all_to_all(outbound, 'gx', split_axis=0, concat_axis=0, tiled=True)]
    ppermute x0 -> x5, starting transfers between devices: none -> 6.55 us  [the longest x2 4.96 us: on_device(): arrived_other = lax.ppermute(arrived, 'gy', pair_r)]
    convert_element_type x0 -> x4, other arithmetic: none -> 6.07 us  [the longest x2 3.13 us: lent_scores(): (row_valid[None, :, :] & jnp.transpose(listed)[:, :, None]).astype(jnp.in...]
  transfers between devices with their start and end apart: 4 -> 8, of which waited for: 4 -> 4; matrix products, arithmetic and copies ran while one was open for 12% -> 11% of each run, Pallas kernels for 0% -> 15%
where the time goes in v2:
time: 154 us; the launch traced here: 153 us
  Pallas kernels  45.3 us (29%)
  waiting for transfers between devices  42.2 us (27%)
  starting transfers between devices  34.5 us (22%)
  other arithmetic  15.1 us (10%)
  local copies, waits for them, and re-layouts  14.9 us (10%)
    pallas_call x8, Pallas kernels, lent_scores(): pl.pallas_call(_score_kernel, out_shape=(jax.ShapeDtypeStruct((n_rows, 12...  45.3 us
    all_to_all x2, waiting for transfers between devices, on_device(): lax.all_to_all(outbound, 'gx', split_axis=0, concat_axis=0, tiled=True)  30.3 us
    all_to_all x2, starting transfers between devices, on_device(): lax.all_to_all(outbound, 'gx', split_axis=0, concat_axis=0, tiled=True)  19.2 us
    all_to_all x1, waiting for transfers between devices, on_device(): lax.all_to_all(row_mine, 'gx', split_axis=1, concat_axis=1, tiled=True)  9.95 us
    all_to_all x1, starting transfers between devices, on_device(): lax.all_to_all(row_mine, 'gx', split_axis=1, concat_axis=1, tiled=True)  8.78 us
    gather x2, local copies, waits for them, and re-layouts, on_device(): outbound = own_pieces[outgoing_sent_block, outgoing_sent_piece]  6.95 us
    ppermute x2, starting transfers between devices, on_device(): arrived_other = lax.ppermute(arrived, 'gy', pair_r)  4.96 us
    convert_element_type x2, other arithmetic, lent_scores(): (row_valid[None, :, :] & jnp.transpose(listed)[:, :, None]).astype(jnp.in...  3.13 us
  transfers between devices with their start and end apart: 8, of which 4 were waited for; matrix products, arithmetic and copies ran while one was open for 11% of the time, Pallas kernels for 15%

profile of v2, /device:TPU:1, one launch (start us, length us, event | category | flops | bytes accessed | tf_op | source)
XLA Modules:
  0.0 152.6 jit_solution(8680499314211865974)
XLA Ops:
  0.9 2.6 %fusion = f32[4,512]{1,0:T(4,128)S(1)} fusion(bf16[4,512,768]{2,1,0:T(8,128)(2,1)} %param.4), kind=kLoop, calls=%fused_computation.6 | loop fusion | flops 4716544 | bytes 3153920 | tf_op jit(solution)/shard_map/reduce_sum | solution.py:16
  3.6 2.3 %fusion.33 = bf16[4,64,8,768]{3,2,1,0:T(8,128)(2,1)} fusion(f32[4,512]{1,0:T(4,128)S(1)} %add_rsqrt_fusion, bf16[4,512,768]{2,1,0:T(8,128)(2,1)S(1)} %copy-done.1), kind=kLoop, calls=%fused_computation.131 | loop fusion | flops 4718592 | bytes 6299648 | tf_op jit(solution)/shard_map/reshape | solution.py:92
  6.1 3.5 %gather_fusion.3 = bf16[64,8,768]{2,1,0:T(8,128)(2,1)} fusion(bf16[4,64,8,768]{3,2,1,0:T(8,128)(2,1)} %fusion.33, s32[64]{0:T(128)S(1)} %fusion.26), kind=kCustom, calls=%fused_computation.3 | custom fusion | bytes 1573376 | tf_op jit(solution)/shard_map/gather | solution.py:113
  9.5 13.3 %all-to-all-start.1 = ((bf16[64,8,768]{2,1,0:T(8,128)(2,1)}), bf16[64,8,768]{2,1,0:T(8,128)(2,1)}, u32[]{:S(2)}, u32[]{:S(2)}) async-start(bf16[64,8,768]{2,1,0:T(8,128)(2,1)} %gather_fusion.3), calls=%async_computation.1 | async-start | bytes 1572864 | tf_op jit(solution)/shard_map/all_to_all | solution.py:114
  22.9 2.3 %fusion.1 = bf16[4,512,768]{2,1,0:T(8,128)(2,1)} fusion(bf16[4,512,768]{2,1,0:T(8,128)(2,1)S(1)} %copy-done.1, f32[4,512]{1,0:T(4,128)S(1)} %add_rsqrt_fusion), kind=kLoop, calls=%fused_computation.7 | loop fusion | flops 4718592 | bytes 6299648 | tf_op jit(solution)/shard_map/convert_element_type | solution.py:16
  26.6 3.5 %gather_fusion.1 = bf16[64,8,768]{2,1,0:T(8,128)(2,1)} fusion(bf16[4,64,8,768]{3,2,1,0:T(8,128)(2,1)} %fusion.33, s32[64]{0:T(128)S(1)} %fusion.27), kind=kCustom, calls=%fused_computation.1 | custom fusion | bytes 1573376 | tf_op jit(solution)/shard_map/gather | solution.py:113
  30.4 15.4 %all-to-all-done.1 = bf16[64,8,768]{2,1,0:T(8,128)(2,1)} async-done(((bf16[64,8,768]{2,1,0:T(8,128)(2,1)}), bf16[64,8,768]{2,1,0:T(8,128)(2,1)}, u32[]{:S(2)}, u32[]{:S(2)}) %all-to-all-start.1) | async-done | bytes 786464 | tf_op jit(solution)/shard_map/all_to_all | solution.py:114
  45.8 5.9 %all-to-all-start = ((bf16[64,8,768]{2,1,0:T(8,128)(2,1)}), bf16[64,8,768]{2,1,0:T(8,128)(2,1)S(1)}, u32[]{:S(2)}, u32[]{:S(2)}) async-start(bf16[64,8,768]{2,1,0:T(8,128)(2,1)} %gather_fusion.1), calls=%async_computation | async-start | bytes 1572864 | tf_op jit(solution)/shard_map/all_to_all | solution.py:114
  55.1 1.6 %and_convert_fusion.2 = (s32[4,512,1]{2,1,0:T(8,128)}, s32[4,512,1]{2,1,0:T(8,128)}) fusion(pred[4,512,1]{2,1,0:T(8,128)(4,1)S(1)} %and.349, pred[512]{0:T(512)(128)(4,1)S(1)} %get-tuple-element.52, pred[512]{0:T(512)(128)(4,1)S(1)} %get-tuple-element.51), kind=kLoop, calls=%fused_computation.12 | loop fusion | flops 8192 | bytes 19456 | tf_op jit(solution)/shard_map/convert_element_type | solution.py:47
  56.7 2.5 %collective-permute-start.2 = (bf16[64,8,768]{2,1,0:T(8,128)(2,1)}, bf16[64,8,768]{2,1,0:T(8,128)(2,1)S(1)}, u32[]{:S(2)}, u32[]{:S(2)}) collective-permute-start(bf16[64,8,768]{2,1,0:T(8,128)(2,1)} %all-to-all-done.1), channel_id=1, source_target_pairs={{0,3},{1,2},{2,1},{3,0},{4,7},{5,6},{6,5},{7,4},{8,11},{9,10},{10,... | collective-permute-start | bytes 2359304 | tf_op jit(solution)/shard_map/ppermute | solution.py:115
  59.8 14.9 %all-to-all-done = bf16[64,8,768]{2,1,0:T(8,128)(2,1)S(1)} async-done(((bf16[64,8,768]{2,1,0:T(8,128)(2,1)}), bf16[64,8,768]{2,1,0:T(8,128)(2,1)S(1)}, u32[]{:S(2)}, u32[]{:S(2)}) %all-to-all-start) | async-done | bytes 786464 | tf_op jit(solution)/shard_map/all_to_all | solution.py:114
  74.7 2.5 %collective-permute-start.1 = (bf16[64,8,768]{2,1,0:T(8,128)(2,1)S(1)}, bf16[64,8,768]{2,1,0:T(8,128)(2,1)S(1)}, u32[]{:S(2)}, u32[]{:S(2)}) collective-permute-start(bf16[64,8,768]{2,1,0:T(8,128)(2,1)S(1)} %all-to-all-done), channel_id=1, source_target_pairs={{0,3},{1,2},{2,1},{3,0},{4,7},{5,6},{6,5},{7,4},{8,11},{9,10},{10,... | collective-permute-start | bytes 2359304 | tf_op jit(solution)/shard_map/ppermute | solution.py:115
  77.7 1.6 %and_convert_fusion.3 = (s32[4,512,1]{2,1,0:T(8,128)}, s32[4,512,1]{2,1,0:T(8,128)}) fusion(pred[4,512,1]{2,1,0:T(8,128)(4,1)S(1)} %and.348, pred[512]{0:T(512)(128)(4,1)S(1)} %get-tuple-element.47, pred[512]{0:T(512)(128)(4,1)S(1)} %get-tuple-element.48), kind=kLoop, calls=%fused_computation.13 | loop fusion | flops 8192 | bytes 19456 | tf_op jit(solution)/shard_map/convert_element_type | solution.py:47
  79.3 5.7 %shard_map.48 = (f32[512,128]{1,0:T(8,128)}, f32[4,1,512]{2,1,0:T(1,128)}) custom-call(s32[4,512,1]{2,1,0:T(8,128)} %get-tuple-element.39.rowmask_ref, s32[4,1,512]{2,1,0:T(1,128)} %get-tuple-element.57.colvalid_ref, bf16[512,768]{1,0:T(8,128)(2,1)} %bitcast.16.lhs_ref, bf16[2048,768]{1,0:T(8,128)(2,1)} %bitcast.8.rhs_ref), custom_call_target="tpu_custom_call" | custom-call | flops 1610612736 | bytes 3932160 | tf_op jit(solution)/shard_map/pallas_call | solution.py:50
  85.0 5.7 %shard_map.46 = (f32[512,128]{1,0:T(8,128)}, f32[4,1,512]{2,1,0:T(1,128)}) custom-call(s32[4,512,1]{2,1,0:T(8,128)} %get-tuple-element.37.rowmask_ref, s32[4,1,512]{2,1,0:T(1,128)} %get-tuple-element.57.colvalid_ref, bf16[512,768]{1,0:T(8,128)(2,1)} %bitcast.95, bf16[2048,768]{1,0:T(8,128)(2,1)} %bitcast.8.rhs_ref), custom_call_target="tpu_custom_call" | custom-call | flops 1610612736 | bytes 3932160 | tf_op jit(solution)/shard_map/pallas_call | solution.py:50
  91.5 5.7 %shard_map.52 = (f32[512,128]{1,0:T(8,128)}, f32[4,1,512]{2,1,0:T(1,128)}) custom-call(s32[4,512,1]{2,1,0:T(8,128)} %get-tuple-element.40.rowmask_ref, s32[4,1,512]{2,1,0:T(1,128)} %get-tuple-element.57.colvalid_ref, bf16[512,768]{1,0:T(8,128)(2,1)} %bitcast.102, bf16[2048,768]{1,0:T(8,128)(2,1)} %bitcast.8.rhs_ref), custom_call_target="tpu_custom_call" | custom-call | flops 1610612736 | bytes 3932160 | tf_op jit(solution)/shard_map/pallas_call | solution.py:50
  98.1 5.7 %shard_map.50 = (f32[512,128]{1,0:T(8,128)}, f32[4,1,512]{2,1,0:T(1,128)}) custom-call(s32[4,512,1]{2,1,0:T(8,128)} %get-tuple-element.38.rowmask_ref, s32[4,1,512]{2,1,0:T(1,128)} %get-tuple-element.57.colvalid_ref, bf16[512,768]{1,0:T(8,128)(2,1)} %bitcast.104, bf16[2048,768]{1,0:T(8,128)(2,1)} %bitcast.8.rhs_ref), custom_call_target="tpu_custom_call" | custom-call | flops 1610612736 | bytes 3932160 | tf_op jit(solution)/shard_map/pallas_call | solution.py:50
  103.8 5.6 %shard_map.53 = (f32[512,128]{1,0:T(8,128)}, f32[4,1,512]{2,1,0:T(1,128)}) custom-call(s32[4,512,1]{2,1,0:T(8,128)} %get-tuple-element.40.rowmask_ref, s32[4,1,512]{2,1,0:T(1,128)} %get-tuple-element.58.colvalid_ref, bf16[512,768]{1,0:T(8,128)(2,1)} %bitcast.103, bf16[2048,768]{1,0:T(8,128)(2,1)} %bitcast.9.rhs_ref), custom_call_target="tpu_custom_call" | custom-call | flops 1610612736 | bytes 3932160 | tf_op jit(solution)/shard_map/pallas_call | solution.py:50
  109.4 5.7 %shard_map.51 = (f32[512,128]{1,0:T(8,128)}, f32[4,1,512]{2,1,0:T(1,128)}) custom-call(s32[4,512,1]{2,1,0:T(8,128)} %get-tuple-element.38.rowmask_ref, s32[4,1,512]{2,1,0:T(1,128)} %get-tuple-element.58.colvalid_ref, bf16[512,768]{1,0:T(8,128)(2,1)} %bitcast.105, bf16[2048,768]{1,0:T(8,128)(2,1)} %bitcast.9.rhs_ref), custom_call_target="tpu_custom_call" | custom-call | flops 1610612736 | bytes 3932160 | tf_op jit(solution)/shard_map/pallas_call | solution.py:50
  115.1 5.6 %shard_map.49 = (f32[512,128]{1,0:T(8,128)}, f32[4,1,512]{2,1,0:T(1,128)}) custom-call(s32[4,512,1]{2,1,0:T(8,128)} %get-tuple-element.39.rowmask_ref, s32[4,1,512]{2,1,0:T(1,128)} %get-tuple-element.58.colvalid_ref, bf16[512,768]{1,0:T(8,128)(2,1)} %bitcast.16.lhs_ref, bf16[2048,768]{1,0:T(8,128)(2,1)} %bitcast.9.rhs_ref), custom_call_target="tpu_custom_call" | custom-call | flops 1610612736 | bytes 3932160 | tf_op jit(solution)/shard_map/pallas_call | solution.py:50
  120.8 5.7 %shard_map.47 = (f32[512,128]{1,0:T(8,128)}, f32[4,1,512]{2,1,0:T(1,128)}) custom-call(s32[4,512,1]{2,1,0:T(8,128)} %get-tuple-element.37.rowmask_ref, s32[4,1,512]{2,1,0:T(1,128)} %get-tuple-element.58.colvalid_ref, bf16[512,768]{1,0:T(8,128)(2,1)} %bitcast.96, bf16[2048,768]{1,0:T(8,128)(2,1)} %bitcast.9.rhs_ref), custom_call_target="tpu_custom_call" | custom-call | flops 1610612736 | bytes 3932160 | tf_op jit(solution)/shard_map/pallas_call | solution.py:50
  129.6 2.0 %collective-permute-done.3 = f32[2,64,8]{2,1,0:T(8,128)S(1)} collective-permute-done((f32[2,64,8]{2,1,0:T(8,128)S(1)}, f32[2,64,8]{2,1,0:T(8,128)S(1)}, u32[]{:S(2)}, u32[]{:S(2)}) %collective-permute-start.3) | collective-permute-done | bytes 4128 | tf_op jit(solution)/shard_map/ppermute | solution.py:135
  132.2 8.8 %all-to-all-start.2 = ((f32[2,64,8]{2,0,1:T(2,128)}), f32[2,64,8]{2,0,1:T(2,128)S(1)}, u32[]{:S(2)}, u32[]{:S(2)}) async-start(f32[2,64,8]{2,0,1:T(2,128)} %copy.71), calls=%async_computation.2 | async-start | bytes 131072 | tf_op jit(solution)/shard_map/all_to_all | solution.py:137
  141.2 9.9 %all-to-all-done.2 = f32[2,64,8]{2,0,1:T(2,128)S(1)} async-done(((f32[2,64,8]{2,0,1:T(2,128)}), f32[2,64,8]{2,0,1:T(2,128)S(1)}, u32[]{:S(2)}, u32[]{:S(2)}) %all-to-all-start.2) | async-done | bytes 4128 | tf_op jit(solution)/shard_map/all_to_all | solution.py:137
  (110 shorter events, 14.4 us)
Async XLA Ops:
  9.5 36.3 %all-to-all-start.1 = ((bf16[64,8,768]{2,1,0:T(8,128)(2,1)}), bf16[64,8,768]{2,1,0:T(8,128)(2,1)}, u32[]{:S(2)}, u32[]{:S(2)}) async-start(bf16[64,8,768]{2,1,0:T(8,128)(2,1)} %gather_fusion.3), calls=%async_computation.1 | async-start | bytes 1572864 | tf_op jit(solution)/shard_map/all_to_all | solution.py:114
  25.1 27.1 %copy-start = (s32[256]{0:T(256)S(1)}, s32[256]{0:T(256)}, u32[]{:S(2)}) copy-start(s32[256]{0:T(256)} %param.7) | copy-start | bytes 3076
  25.1 78.6 %collective-permute-start = (bf16[4,512,768]{2,1,0:T(8,128)(2,1)}, bf16[4,512,768]{2,1,0:T(8,128)(2,1)}, u32[]{:S(2)}, u32[]{:S(2)}) collective-permute-start(bf16[4,512,768]{2,1,0:T(8,128)(2,1)} %fusion.1), channel_id=1, source_target_pairs={{0,1},{1,0},{2,3},{3,2},{4,5},{5,4},{6,7},{7,6},{8,9},{9,8},{10,11... | collective-permute-start | bytes 9437192 | tf_op jit(solution)/shard_map/ppermute | solution.py:91
  45.8 28.9 %all-to-all-start = ((bf16[64,8,768]{2,1,0:T(8,128)(2,1)}), bf16[64,8,768]{2,1,0:T(8,128)(2,1)S(1)}, u32[]{:S(2)}, u32[]{:S(2)}) async-start(bf16[64,8,768]{2,1,0:T(8,128)(2,1)} %gather_fusion.1), calls=%async_computation | async-start | bytes 1572864 | tf_op jit(solution)/shard_map/all_to_all | solution.py:114
  56.7 33.9 %collective-permute-start.2 = (bf16[64,8,768]{2,1,0:T(8,128)(2,1)}, bf16[64,8,768]{2,1,0:T(8,128)(2,1)S(1)}, u32[]{:S(2)}, u32[]{:S(2)}) collective-permute-start(bf16[64,8,768]{2,1,0:T(8,128)(2,1)} %all-to-all-done.1), channel_id=1, source_target_pairs={{0,3},{1,2},{2,1},{3,0},{4,7},{5,6},{6,5},{7,4},{8,11},{9,10},{10,... | collective-permute-start | bytes 2359304 | tf_op jit(solution)/shard_map/ppermute | solution.py:115
  74.7 10.2 %copy-start.2 = (bf16[64,8,768]{2,1,0:T(8,128)(2,1)}, bf16[64,8,768]{2,1,0:T(8,128)(2,1)S(1)}, u32[]{:S(2)}) copy-start(bf16[64,8,768]{2,1,0:T(8,128)(2,1)S(1)} %all-to-all-done) | copy-start | bytes 2359300
  74.7 22.5 %collective-permute-start.1 = (bf16[64,8,768]{2,1,0:T(8,128)(2,1)S(1)}, bf16[64,8,768]{2,1,0:T(8,128)(2,1)S(1)}, u32[]{:S(2)}, u32[]{:S(2)}) collective-permute-start(bf16[64,8,768]{2,1,0:T(8,128)(2,1)S(1)} %all-to-all-done), channel_id=1, source_target_pairs={{0,3},{1,2},{2,1},{3,0},{4,7},{5,6},{6,5},{7,4},{8,11},{9,10},{10,... | collective-permute-start | bytes 2359304 | tf_op jit(solution)/shard_map/ppermute | solution.py:115
  120.7 5.9 %copy-start.5 = (f32[512,128]{1,0:T(8,128)S(1)}, f32[512,128]{1,0:T(8,128)}, u32[]{:S(2)}) copy-start(f32[512,128]{1,0:T(8,128)} %get-tuple-element.27) | copy-start | bytes 786436
  120.7 5.9 %copy-start.8 = (f32[512,128]{1,0:T(8,128)S(1)}, f32[512,128]{1,0:T(8,128)}, u32[]{:S(2)}) copy-start(f32[512,128]{1,0:T(8,128)} %get-tuple-element.28) | copy-start | bytes 786436
  120.7 6.1 %copy-start.6 = (f32[512,128]{1,0:T(8,128)S(1)}, f32[512,128]{1,0:T(8,128)}, u32[]{:S(2)}) copy-start(f32[512,128]{1,0:T(8,128)} %get-tuple-element.25) | copy-start | bytes 786436
  120.7 6.1 %copy-start.9 = (f32[512,128]{1,0:T(8,128)S(1)}, f32[512,128]{1,0:T(8,128)}, u32[]{:S(2)}) copy-start(f32[512,128]{1,0:T(8,128)} %get-tuple-element.26) | copy-start | bytes 786436
  120.8 6.7 %copy-start.4 = (f32[512,128]{1,0:T(8,128)S(1)}, f32[512,128]{1,0:T(8,128)}, u32[]{:S(2)}) copy-start(f32[512,128]{1,0:T(8,128)} %get-tuple-element.23) | copy-start | bytes 786436
  120.8 6.7 %copy-start.7 = (f32[512,128]{1,0:T(8,128)S(1)}, f32[512,128]{1,0:T(8,128)}, u32[]{:S(2)}) copy-start(f32[512,128]{1,0:T(8,128)} %get-tuple-element.24) | copy-start | bytes 786436
  120.8 6.8 %copy-start.12 = (f32[4,1,512]{2,1,0:T(1,128)S(1)}, f32[4,1,512]{2,1,0:T(1,128)}, u32[]{:S(2)}) copy-start(f32[4,1,512]{2,1,0:T(1,128)} %get-tuple-element.34) | copy-start | bytes 24580
  120.8 6.8 %copy-start.13 = (f32[4,1,512]{2,1,0:T(1,128)S(1)}, f32[4,1,512]{2,1,0:T(1,128)}, u32[]{:S(2)}) copy-start(f32[4,1,512]{2,1,0:T(1,128)} %get-tuple-element.35) | copy-start | bytes 24580
  120.8 7.5 %copy-start.3 = (f32[512,128]{1,0:T(8,128)S(1)}, f32[512,128]{1,0:T(8,128)}, u32[]{:S(2)}) copy-start(f32[512,128]{1,0:T(8,128)} %get-tuple-element.21) | copy-start | bytes 786436
  120.8 20.2 %copy-start.11 = (f32[4,1,512]{2,1,0:T(1,128)S(1)}, f32[4,1,512]{2,1,0:T(1,128)}, u32[]{:S(2)}) copy-start(f32[4,1,512]{2,1,0:T(1,128)} %get-tuple-element.36) | copy-start | bytes 24580
  126.5 25.3 %copy-start.14 = (f32[4,1,512]{2,1,0:T(1,128)S(1)}, f32[4,1,512]{2,1,0:T(1,128)}, u32[]{:S(2)}) copy-start(f32[4,1,512]{2,1,0:T(1,128)} %get-tuple-element.31) | copy-start | bytes 24580
  126.5 25.4 %copy-start.15 = (f32[4,1,512]{2,1,0:T(1,128)S(1)}, f32[4,1,512]{2,1,0:T(1,128)}, u32[]{:S(2)}) copy-start(f32[4,1,512]{2,1,0:T(1,128)} %get-tuple-element.29) | copy-start | bytes 24580
  126.6 25.4 %copy-start.16 = (f32[4,1,512]{2,1,0:T(1,128)S(1)}, f32[4,1,512]{2,1,0:T(1,128)}, u32[]{:S(2)}) copy-start(f32[4,1,512]{2,1,0:T(1,128)} %get-tuple-element.32) | copy-start | bytes 24580
  126.6 25.4 %copy-start.17 = (f32[4,1,512]{2,1,0:T(1,128)S(1)}, f32[4,1,512]{2,1,0:T(1,128)}, u32[]{:S(2)}) copy-start(f32[4,1,512]{2,1,0:T(1,128)} %get-tuple-element.30) | copy-start | bytes 24580
  127.1 4.4 %collective-permute-start.3 = (f32[2,64,8]{2,1,0:T(8,128)S(1)}, f32[2,64,8]{2,1,0:T(8,128)S(1)}, u32[]{:S(2)}, u32[]{:S(2)}) collective-permute-start(f32[2,64,8]{2,1,0:T(8,128)S(1)} %pad_maximum_fusion), channel_id=1, source_target_pairs={{0,3},{1,2},{2,1},{3,0},{4,7},{5,6},{6,5},{7,4},{8,11},{9,10},{10,... | collective-permute-start | bytes 12296 | tf_op jit(solution)/shard_map/ppermute | solution.py:135
  132.2 18.9 %all-to-all-start.2 = ((f32[2,64,8]{2,0,1:T(2,128)}), f32[2,64,8]{2,0,1:T(2,128)S(1)}, u32[]{:S(2)}, u32[]{:S(2)}) async-start(f32[2,64,8]{2,0,1:T(2,128)} %copy.71), calls=%async_computation.2 | async-start | bytes 131072 | tf_op jit(solution)/shard_map/all_to_all | solution.py:137
  141.1 10.8 %collective-permute-start.4 = (f32[4,512]{1,0:T(4,128)S(1)}, f32[4,512]{1,0:T(4,128)S(1)}, u32[]{:S(2)}, u32[]{:S(2)}) collective-permute-start(f32[4,512]{1,0:T(4,128)S(1)} %bitcast.99), channel_id=1, source_target_pairs={{0,1},{1,0},{2,3},{3,2},{4,5},{5,4},{6,7},{7,6},{8,9},{9,8},{10,11... | collective-permute-start | bytes 24584 | tf_op jit(solution)/shard_map/ppermute | solution.py:132
  (4 other events, 8.9 us)

commit v3 on v2

--- a/solution.py
+++ b/solution.py
@@ -18,59 +18,72 @@
     )
 
 
-def _score_kernel(rowmask_ref, colvalid_ref, lhs_ref, rhs_ref, rowmax_ref, colmax_ref):
+def _score_kernel(limit_ref, rowmask_ref, lhs_ref, rhs_ref, rowmax_ref, colmax_ref, acc_ref):
     step = pl.program_id(0)
     scores = lax.dot_general(
-        lhs_ref[...], rhs_ref[...], (((1,), (1,)), ((), ())), preferred_element_type=jnp.float32
+        lhs_ref[...], rhs_ref[0], (((1,), (1,)), ((), ())), preferred_element_type=jnp.float32
     )
-    keep = (rowmask_ref[0] > 0) & (colvalid_ref[0] > 0)
-    scores = jnp.where(keep, scores, jnp.float32(-1.0))
-    row_best = jnp.max(scores, axis=1, keepdims=True)
+    n_rows, n_cols = scores.shape
+    lanes = rowmask_ref.shape[-1]
+    row_keep = rowmask_ref[0] > 0
+    row_keep = jnp.concatenate([row_keep] * (n_cols // lanes), axis=1)
+    col_keep = lax.broadcasted_iota(jnp.int32, (1, n_cols), 1) < limit_ref[step]
+    scores = jnp.where(row_keep & col_keep, scores, jnp.float32(-1.0))
     colmax_ref[0] = jnp.max(scores, axis=0, keepdims=True)
+    part = scores[:, 0:lanes]
+    for start in range(lanes, n_cols, lanes):
+        part = jnp.maximum(part, scores[:, start : start + lanes])
 
     @pl.when(step == 0)
     def _():
-        rowmax_ref[...] = jnp.broadcast_to(row_best, rowmax_ref.shape)
+        acc_ref[...] = part
 
     @pl.when(step > 0)
     def _():
-        rowmax_ref[...] = jnp.maximum(rowmax_ref[...], row_best)
+        acc_ref[...] = jnp.maximum(acc_ref[...], part)
+
+    @pl.when(step == pl.num_programs(0) - 1)
+    def _():
+        rowmax_ref[...] = jnp.broadcast_to(
+            jnp.max(acc_ref[...], axis=1, keepdims=True), rowmax_ref.shape
+        )
 
 
-def lent_scores(lent, row_valid, listed, columns, col_valid):
+def lent_scores(lent, row_valid, listed, columns, col_limit):
     slots, lent_rows, width = lent.shape
     owned, quarter, _ = columns.shape
     n_rows = slots * lent_rows
-    tiles = owned
+    lanes = 128
     flat_rows = lent.reshape(n_rows, width)
-    flat_cols = columns.reshape(tiles * quarter, width)
     rowmask = (row_valid[None, :, :] & jnp.transpose(listed)[:, :, None]).astype(jnp.int32)
-    rowmask = rowmask.reshape(owned, n_rows, 1)
-    colmask = col_valid.astype(jnp.int32).reshape(tiles, 1, quarter)
+    rowmask = jnp.broadcast_to(rowmask.reshape(owned, n_rows, 1), (owned, n_rows, lanes))
     rowmax, colmax = pl.pallas_call(
         _score_kernel,
         out_shape=(
-            jax.ShapeDtypeStruct((n_rows, 128), jnp.float32),
-            jax.ShapeDtypeStruct((tiles, 1, quarter), jnp.float32),
+            jax.ShapeDtypeStruct((n_rows, lanes), jnp.float32),
+            jax.ShapeDtypeStruct((owned, 1, quarter), jnp.float32),
         ),
-        grid=(tiles,),
-        in_specs=[
-            pl.BlockSpec((1, n_rows, 1), lambda j: (j, 0, 0)),
-            pl.BlockSpec((1, 1, quarter), lambda j: (j, 0, 0)),
-            pl.BlockSpec((n_rows, width), lambda j: (0, 0)),
-            pl.BlockSpec((quarter, width), lambda j: (j, 0)),
-        ],
-        out_specs=[
-            pl.BlockSpec((n_rows, 128), lambda j: (0, 0)),
-            pl.BlockSpec((1, 1, quarter), lambda j: (j, 0, 0)),
-        ],
+        grid_spec=pltpu.PrefetchScalarGridSpec(
+            num_scalar_prefetch=1,
+            grid=(owned,),
+            in_specs=[
+                pl.BlockSpec((1, n_rows, lanes), lambda k, lim: (k, 0, 0)),
+                pl.BlockSpec((n_rows, width), lambda k, lim: (0, 0)),
+                pl.BlockSpec((1, quarter, width), lambda k, lim: (k, 0, 0)),
+            ],
+            out_specs=[
+                pl.BlockSpec((n_rows, lanes), lambda k, lim: (0, 0)),
+                pl.BlockSpec((1, 1, quarter), lambda k, lim: (k, 0, 0)),
+            ],
+            scratch_shapes=[pltpu.VMEM((n_rows, lanes), jnp.float32)],
+        ),
         compiler_params=pltpu.CompilerParams(dimension_semantics=("arbitrary",)),
         cost_estimate=pl.CostEstimate(
-            flops=2 * n_rows * tiles * quarter * width,
+            flops=2 * n_rows * owned * quarter * width,
             transcendentals=0,
-            bytes_accessed=2 * (n_rows + tiles * quarter) * width,
+            bytes_accessed=2 * (n_rows + owned * quarter) * width + 4 * owned * n_rows * lanes,
         ),
-    )(rowmask, colmask, flat_rows, flat_cols)
+    )(col_limit, rowmask, flat_rows, columns)
     return rowmax[:, 0].reshape(slots, lent_rows), colmax.reshape(owned, quarter)
 
 
@@ -94,8 +107,8 @@
     positions = jnp.arange(quarter, dtype=jnp.int32)
     col_sources = []
     for lane, unit in ((my_lane, own_unit), (lane_p, other_unit)):
-        col_valid = (lane * quarter + positions)[None, :] < own_counts[:, None]
-        col_sources.append((unit, col_valid))
+        col_limit = (own_counts - lane * quarter).astype(jnp.int32)
+        col_sources.append((unit, col_limit))
     slice_offsets = jnp.arange(slice_rows, dtype=jnp.int32)
     local_ids = jnp.arange(owned, dtype=jnp.int32)
     piece_ids = jnp.arange(pieces, dtype=jnp.int32)
@@ -124,8 +137,8 @@
         ):
             row_valid = (lane * quarter + piece_rows) < arrived_counts[:, None]
             row_best = jnp.full(row_valid.shape, -1.0, jnp.float32)
-            for source, (unit, col_valid) in enumerate(col_sources):
-                rows_max, col_best = lent_scores(rows_in, row_valid, listed, unit, col_valid)
+            for source, (unit, col_limit) in enumerate(col_sources):
+                rows_max, col_best = lent_scores(rows_in, row_valid, listed, unit, col_limit)
                 row_best = jnp.maximum(row_best, rows_max)
                 col_part[source] = jnp.maximum(col_part[source], col_best)
             parts.append(row_best)

time: 154 us -> 159 us (1.032)
  Pallas kernels: 45.3 us -> 50.4 us
  local copies, waits for them, and re-layouts: 14.9 us -> 17.8 us
  starting transfers between devices: 34.5 us -> 32.5 us
    broadcast_in_dim x0 -> x4, local copies, waits for them, and re-layouts: none -> 5.4 us  [lent_scores(): jnp.broadcast_to(rowmask.reshape(owned, n_rows, 1), (owned, n_rows, lanes))]
    pallas_call x8, Pallas kernels: 45.3 us -> 50.4 us  [lent_scores(): pl.pallas_call(_score_kernel, out_shape=(jax.ShapeDtypeStruct((n_rows, la...]
    convert_element_type x2, other arithmetic: 3.13 us -> 0.02 us  [lent_scores(): (row_valid[None, :, :] & jnp.transpose(listed)[:, :, None]).astype(jnp.in...]
    max x4, other arithmetic: 1.54 us -> 4.52 us  [on_device(): row_best = jnp.maximum(row_best, rows_max)]
    all_to_all x1, starting transfers between devices: 8.78 us -> 6.46 us  [on_device(): lax.all_to_all(row_mine, 'gx', split_axis=1, concat_axis=1, tiled=True)]
    ppermute x1, waiting for transfers between devices: 1.96 us -> 0.01 us  [on_device(): row_back = lax.ppermute(row_other, 'gy', pair_r)]
    unnamed x41 -> x35, local copies, waits for them, and re-layouts: 1.9 us -> 0.08 us
  transfers between devices with their start and end apart: 8 -> 8, of which waited for: 4 -> 3; matrix products, arithmetic and copies ran while one was open for 11% -> 13% of each run, Pallas kernels for 15% -> 24%
where the time goes in v3:
time: 159 us; the launch traced here: 158 us
  Pallas kernels  50.4 us (32%)
  waiting for transfers between devices  41.5 us (26%)
  starting transfers between devices  32.5 us (20%)
  local copies, waits for them, and re-layouts  17.8 us (11%)
  other arithmetic  15.5 us (10%)
    pallas_call x8, Pallas kernels, lent_scores(): pl.pallas_call(_score_kernel, out_shape=(jax.ShapeDtypeStruct((n_rows, la...  50.4 us
    all_to_all x2, waiting for transfers between devices, on_device(): lax.all_to_all(outbound, 'gx', split_axis=0, concat_axis=0, tiled=True)  31.5 us
    all_to_all x2, starting transfers between devices, on_device(): lax.all_to_all(outbound, 'gx', split_axis=0, concat_axis=0, tiled=True)  19.2 us
    all_to_all x1, waiting for transfers between devices, on_device(): lax.all_to_all(row_mine, 'gx', split_axis=1, concat_axis=1, tiled=True)  9.95 us
    gather x2, local copies, waits for them, and re-layouts, on_device(): outbound = own_pieces[outgoing_sent_block, outgoing_sent_piece]  6.96 us
    all_to_all x1, starting transfers between devices, on_device(): lax.all_to_all(row_mine, 'gx', split_axis=1, concat_axis=1, tiled=True)  6.46 us
    broadcast_in_dim x4, local copies, waits for them, and re-layouts, lent_scores(): jnp.broadcast_to(rowmask.reshape(owned, n_rows, 1), (owned, n_rows, lanes))  5.4 us
    ppermute x2, starting transfers between devices, on_device(): arrived_other = lax.ppermute(arrived, 'gy', pair_r)  5.04 us
  transfers between devices with their start and end apart: 8, of which 3 were waited for; matrix products, arithmetic and copies ran while one was open for 13% of the time, Pallas kernels for 24%

profile of v3, /device:TPU:1, one launch (start us, length us, event | category | flops | bytes accessed | tf_op | source)
XLA Modules:
  0.0 158.2 jit_solution(4020603130286751624)
XLA Ops:
  0.9 2.6 %fusion = f32[4,512]{1,0:T(4,128)S(1)} fusion(bf16[4,512,768]{2,1,0:T(8,128)(2,1)} %param.4), kind=kLoop, calls=%fused_computation.6 | loop fusion | flops 4716544 | bytes 3153920 | tf_op jit(solution)/shard_map/reduce_sum | solution.py:16
  3.6 2.3 %fusion.33 = bf16[4,64,8,768]{3,2,1,0:T(8,128)(2,1)} fusion(f32[4,512]{1,0:T(4,128)S(1)} %add_rsqrt_fusion, bf16[4,512,768]{2,1,0:T(8,128)(2,1)S(1)} %copy-done.1), kind=kLoop, calls=%fused_computation.130 | loop fusion | flops 4718592 | bytes 6299648 | tf_op jit(solution)/shard_map/reshape | solution.py:105
  6.1 3.5 %gather_fusion.3 = bf16[64,8,768]{2,1,0:T(8,128)(2,1)} fusion(bf16[4,64,8,768]{3,2,1,0:T(8,128)(2,1)} %fusion.33, s32[64]{0:T(128)S(1)} %fusion.26), kind=kCustom, calls=%fused_computation.3 | custom fusion | bytes 1573376 | tf_op jit(solution)/shard_map/gather | solution.py:126
  9.6 13.3 %all-to-all-start.1 = ((bf16[64,8,768]{2,1,0:T(8,128)(2,1)}), bf16[64,8,768]{2,1,0:T(8,128)(2,1)}, u32[]{:S(2)}, u32[]{:S(2)}) async-start(bf16[64,8,768]{2,1,0:T(8,128)(2,1)} %gather_fusion.3), calls=%async_computation.1 | async-start | bytes 1572864 | tf_op jit(solution)/shard_map/all_to_all | solution.py:127
  22.9 2.2 %fusion.1.rhs_ref = bf16[4,512,768]{2,1,0:T(8,128)(2,1)} fusion(bf16[4,512,768]{2,1,0:T(8,128)(2,1)S(1)} %copy-done.1, f32[4,512]{1,0:T(4,128)S(1)} %add_rsqrt_fusion), kind=kLoop, calls=%fused_computation.7 | loop fusion | flops 4718592 | bytes 6299648 | tf_op jit(solution)/shard_map/convert_element_type | solution.py:16
  29.6 3.5 %gather_fusion.1 = bf16[64,8,768]{2,1,0:T(8,128)(2,1)} fusion(bf16[4,64,8,768]{3,2,1,0:T(8,128)(2,1)} %fusion.33, s32[64]{0:T(128)S(1)} %fusion.27), kind=kCustom, calls=%fused_computation.1 | custom fusion | bytes 1573376 | tf_op jit(solution)/shard_map/gather | solution.py:126
  33.8 12.0 %all-to-all-done.1 = bf16[64,8,768]{2,1,0:T(8,128)(2,1)} async-done(((bf16[64,8,768]{2,1,0:T(8,128)(2,1)}), bf16[64,8,768]{2,1,0:T(8,128)(2,1)}, u32[]{:S(2)}, u32[]{:S(2)}) %all-to-all-start.1) | async-done | bytes 786464 | tf_op jit(solution)/shard_map/all_to_all | solution.py:127
  45.8 5.9 %all-to-all-start = ((bf16[64,8,768]{2,1,0:T(8,128)(2,1)}), bf16[64,8,768]{2,1,0:T(8,128)(2,1)S(1)}, u32[]{:S(2)}, u32[]{:S(2)}) async-start(bf16[64,8,768]{2,1,0:T(8,128)(2,1)} %gather_fusion.1), calls=%async_computation | async-start | bytes 1572864 | tf_op jit(solution)/shard_map/all_to_all | solution.py:127
  52.1 2.6 %collective-permute-start.2 = (bf16[64,8,768]{2,1,0:T(8,128)(2,1)}, bf16[64,8,768]{2,1,0:T(8,128)(2,1)S(1)}, u32[]{:S(2)}, u32[]{:S(2)}) collective-permute-start(bf16[64,8,768]{2,1,0:T(8,128)(2,1)} %all-to-all-done.1), channel_id=1, source_target_pairs={{0,3},{1,2},{2,1},{3,0},{4,7},{5,6},{6,5},{7,4},{8,11},{9,10},{10,... | collective-permute-start | bytes 2359304 | tf_op jit(solution)/shard_map/ppermute | solution.py:128
  55.2 19.5 %all-to-all-done = bf16[64,8,768]{2,1,0:T(8,128)(2,1)S(1)} async-done(((bf16[64,8,768]{2,1,0:T(8,128)(2,1)}), bf16[64,8,768]{2,1,0:T(8,128)(2,1)S(1)}, u32[]{:S(2)}, u32[]{:S(2)}) %all-to-all-start) | async-done | bytes 786464 | tf_op jit(solution)/shard_map/all_to_all | solution.py:127
  74.7 2.5 %collective-permute-start.1 = (bf16[64,8,768]{2,1,0:T(8,128)(2,1)S(1)}, bf16[64,8,768]{2,1,0:T(8,128)(2,1)S(1)}, u32[]{:S(2)}, u32[]{:S(2)}) collective-permute-start(bf16[64,8,768]{2,1,0:T(8,128)(2,1)S(1)} %all-to-all-done), channel_id=1, source_target_pairs={{0,3},{1,2},{2,1},{3,0},{4,7},{5,6},{6,5},{7,4},{8,11},{9,10},{10,... | collective-permute-start | bytes 2359304 | tf_op jit(solution)/shard_map/ppermute | solution.py:128
  77.4 1.4 broadcast_in_dim.45.rowmask_ref
  78.7 6.3 %shard_map.48 = (f32[512,128]{1,0:T(8,128)}, f32[4,1,512]{2,1,0:T(1,128)}) custom-call(s32[4]{0:T(128)} %get-tuple-element.37.limit_ref, s32[4,512,128]{2,1,0:T(8,128)} %broadcast_in_dim.45.rowmask_ref, bf16[512,768]{1,0:T(8,128)(2,1)} %bitcast.14.lhs_ref, bf16[4,512,768]{2,1,0:T(8,128)(2,1)} %fusion.1.rhs_ref), custom_call_target="tpu_custom_call" | custom-call | flops 1610612736 | bytes 4980736 | tf_op jit(solution)/shard_map/pallas_call | solution.py:60
  85.0 1.3 broadcast_in_dim.44.rowmask_ref
  86.3 6.2 %shard_map.46 = (f32[512,128]{1,0:T(8,128)}, f32[4,1,512]{2,1,0:T(1,128)}) custom-call(s32[4]{0:T(128)} %get-tuple-element.37.limit_ref, s32[4,512,128]{2,1,0:T(8,128)} %broadcast_in_dim.44.rowmask_ref, bf16[512,768]{1,0:T(8,128)(2,1)} %bitcast.93, bf16[4,512,768]{2,1,0:T(8,128)(2,1)} %fusion.1.rhs_ref), custom_call_target="tpu_custom_call" | custom-call | flops 1610612736 | bytes 4980736 | tf_op jit(solution)/shard_map/pallas_call | solution.py:60
  93.9 6.3 %shard_map.52 = (f32[512,128]{1,0:T(8,128)}, f32[4,1,512]{2,1,0:T(1,128)}) custom-call(s32[4]{0:T(128)} %get-tuple-element.37.limit_ref, s32[4,512,128]{2,1,0:T(8,128)} %broadcast_in_dim.47.rowmask_ref, bf16[512,768]{1,0:T(8,128)(2,1)} %bitcast.100, bf16[4,512,768]{2,1,0:T(8,128)(2,1)} %fusion.1.rhs_ref), custom_call_target="tpu_custom_call" | custom-call | flops 1610612736 | bytes 4980736 | tf_op jit(solution)/shard_map/pallas_call | solution.py:60
  100.2 1.4 broadcast_in_dim.46.rowmask_ref
  101.6 6.3 %shard_map.50 = (f32[512,128]{1,0:T(8,128)}, f32[4,1,512]{2,1,0:T(1,128)}) custom-call(s32[4]{0:T(128)} %get-tuple-element.37.limit_ref, s32[4,512,128]{2,1,0:T(8,128)} %broadcast_in_dim.46.rowmask_ref, bf16[512,768]{1,0:T(8,128)(2,1)} %bitcast.102, bf16[4,512,768]{2,1,0:T(8,128)(2,1)} %fusion.1.rhs_ref), custom_call_target="tpu_custom_call" | custom-call | flops 1610612736 | bytes 4980736 | tf_op jit(solution)/shard_map/pallas_call | solution.py:60
  107.8 6.4 %shard_map.53 = (f32[512,128]{1,0:T(8,128)}, f32[4,1,512]{2,1,0:T(1,128)}) custom-call(s32[4]{0:T(128)} %broadcast_subtract_fusion.limit_ref, s32[4,512,128]{2,1,0:T(8,128)} %broadcast_in_dim.47.rowmask_ref, bf16[512,768]{1,0:T(8,128)(2,1)} %bitcast.101, bf16[4,512,768]{2,1,0:T(8,128)(2,1)} %collective-permute-done.rhs_ref), custom_call_target="tpu_custom_call" | custom-call | flops 1610612736 | bytes 4980736 | tf_op jit(solution)/shard_map/pallas_call | solution.py:60
  115.5 6.3 %shard_map.51 = (f32[512,128]{1,0:T(8,128)}, f32[4,1,512]{2,1,0:T(1,128)}) custom-call(s32[4]{0:T(128)} %broadcast_subtract_fusion.limit_ref, s32[4,512,128]{2,1,0:T(8,128)} %broadcast_in_dim.46.rowmask_ref, bf16[512,768]{1,0:T(8,128)(2,1)} %bitcast.103, bf16[4,512,768]{2,1,0:T(8,128)(2,1)} %collective-permute-done.rhs_ref), custom_call_target="tpu_custom_call" | custom-call | flops 1610612736 | bytes 4980736 | tf_op jit(solution)/shard_map/pallas_call | solution.py:60
  123.5 6.3 %shard_map.49 = (f32[512,128]{1,0:T(8,128)}, f32[4,1,512]{2,1,0:T(1,128)}) custom-call(s32[4]{0:T(128)} %broadcast_subtract_fusion.limit_ref, s32[4,512,128]{2,1,0:T(8,128)} %broadcast_in_dim.45.rowmask_ref, bf16[512,768]{1,0:T(8,128)(2,1)} %bitcast.14.lhs_ref, bf16[4,512,768]{2,1,0:T(8,128)(2,1)} %collective-permute-done.rhs_ref), custom_call_target="tpu_custom_call" | custom-call | flops 1610612736 | bytes 4980736 | tf_op jit(solution)/shard_map/pallas_call | solution.py:60
  131.0 6.4 %shard_map.47 = (f32[512,128]{1,0:T(8,128)}, f32[4,1,512]{2,1,0:T(1,128)}) custom-call(s32[4]{0:T(128)} %broadcast_subtract_fusion.limit_ref, s32[4,512,128]{2,1,0:T(8,128)} %broadcast_in_dim.44.rowmask_ref, bf16[512,768]{1,0:T(8,128)(2,1)} %bitcast.94, bf16[4,512,768]{2,1,0:T(8,128)(2,1)} %collective-permute-done.rhs_ref), custom_call_target="tpu_custom_call" | custom-call | flops 1610612736 | bytes 4980736 | tf_op jit(solution)/shard_map/pallas_call | solution.py:60
  140.1 6.5 %all-to-all-start.2 = ((f32[2,64,8]{2,0,1:T(2,128)}), f32[2,64,8]{2,0,1:T(2,128)S(1)}, u32[]{:S(2)}, u32[]{:S(2)}) async-start(f32[2,64,8]{2,0,1:T(2,128)} %copy.41), calls=%async_computation.2 | async-start | bytes 131072 | tf_op jit(solution)/shard_map/all_to_all | solution.py:150
  146.7 9.9 %all-to-all-done.2 = f32[2,64,8]{2,0,1:T(2,128)S(1)} async-done(((f32[2,64,8]{2,0,1:T(2,128)}), f32[2,64,8]{2,0,1:T(2,128)S(1)}, u32[]{:S(2)}, u32[]{:S(2)}) %all-to-all-start.2) | async-done | bytes 4128 | tf_op jit(solution)/shard_map/all_to_all | solution.py:150
  (107 shorter events, 16.9 us)
Async XLA Ops:
  0.0 3.6 %copy-start.1 = (bf16[4,512,768]{2,1,0:T(8,128)(2,1)S(1)}, bf16[4,512,768]{2,1,0:T(8,128)(2,1)}, u32[]{:S(2)}) copy-start(bf16[4,512,768]{2,1,0:T(8,128)(2,1)} %param.4) | copy-start | bytes 9437188
  9.6 36.3 %all-to-all-start.1 = ((bf16[64,8,768]{2,1,0:T(8,128)(2,1)}), bf16[64,8,768]{2,1,0:T(8,128)(2,1)}, u32[]{:S(2)}, u32[]{:S(2)}) async-start(bf16[64,8,768]{2,1,0:T(8,128)(2,1)} %gather_fusion.3), calls=%async_computation.1 | async-start | bytes 1572864 | tf_op jit(solution)/shard_map/all_to_all | solution.py:127
  22.9 3.5 %copy-start.7 = (s32[2,64,64,2]{2,3,1,0:T(2,128)S(1)}, s32[2,64,64,2]{2,3,1,0:T(2,128)}, u32[]{:S(2)}) copy-start(s32[2,64,64,2]{2,3,1,0:T(2,128)} %param.6) | copy-start | bytes 196612
  22.9 3.8 %copy-start = (s32[256]{0:T(256)S(1)}, s32[256]{0:T(256)}, u32[]{:S(2)}) copy-start(s32[256]{0:T(256)} %param.7) | copy-start | bytes 3076
  25.2 82.7 %collective-permute-start = (bf16[4,512,768]{2,1,0:T(8,128)(2,1)}, bf16[4,512,768]{2,1,0:T(8,128)(2,1)}, u32[]{:S(2)}, u32[]{:S(2)}) collective-permute-start(bf16[4,512,768]{2,1,0:T(8,128)(2,1)} %fusion.1.rhs_ref), channel_id=1, source_target_pairs={{0,1},{1,0},{2,3},{3,2},{4,5},{5,4},{6,7},{7,6},{8,9},{9,8},{10,11... | collective-permute-start | bytes 9437192 | tf_op jit(solution)/shard_map/ppermute | solution.py:104
  45.8 28.9 %all-to-all-start = ((bf16[64,8,768]{2,1,0:T(8,128)(2,1)}), bf16[64,8,768]{2,1,0:T(8,128)(2,1)S(1)}, u32[]{:S(2)}, u32[]{:S(2)}) async-start(bf16[64,8,768]{2,1,0:T(8,128)(2,1)} %gather_fusion.1), calls=%async_computation | async-start | bytes 1572864 | tf_op jit(solution)/shard_map/all_to_all | solution.py:127
  52.1 40.5 %collective-permute-start.2 = (bf16[64,8,768]{2,1,0:T(8,128)(2,1)}, bf16[64,8,768]{2,1,0:T(8,128)(2,1)S(1)}, u32[]{:S(2)}, u32[]{:S(2)}) collective-permute-start(bf16[64,8,768]{2,1,0:T(8,128)(2,1)} %all-to-all-done.1), channel_id=1, source_target_pairs={{0,3},{1,2},{2,1},{3,0},{4,7},{5,6},{6,5},{7,4},{8,11},{9,10},{10,... | collective-permute-start | bytes 2359304 | tf_op jit(solution)/shard_map/ppermute | solution.py:128
  74.7 10.2 %copy-start.2 = (bf16[64,8,768]{2,1,0:T(8,128)(2,1)}, bf16[64,8,768]{2,1,0:T(8,128)(2,1)S(1)}, u32[]{:S(2)}) copy-start(bf16[64,8,768]{2,1,0:T(8,128)(2,1)S(1)} %all-to-all-done) | copy-start | bytes 2359300
  74.7 25.4 %collective-permute-start.1 = (bf16[64,8,768]{2,1,0:T(8,128)(2,1)S(1)}, bf16[64,8,768]{2,1,0:T(8,128)(2,1)S(1)}, u32[]{:S(2)}, u32[]{:S(2)}) collective-permute-start(bf16[64,8,768]{2,1,0:T(8,128)(2,1)S(1)} %all-to-all-done), channel_id=1, source_target_pairs={{0,3},{1,2},{2,1},{3,0},{4,7},{5,6},{6,5},{7,4},{8,11},{9,10},{10,... | collective-permute-start | bytes 2359304 | tf_op jit(solution)/shard_map/ppermute | solution.py:128
  100.2 1.4 copy-start.16
  107.8 6.4 %copy-start.6 = (f32[512,128]{1,0:T(8,128)S(1)}, f32[512,128]{1,0:T(8,128)}, u32[]{:S(2)}) copy-start(f32[512,128]{1,0:T(8,128)} %get-tuple-element.27) | copy-start | bytes 786436
  114.2 7.5 %copy-start.5 = (f32[512,128]{1,0:T(8,128)S(1)}, f32[512,128]{1,0:T(8,128)}, u32[]{:S(2)}) copy-start(f32[512,128]{1,0:T(8,128)} %get-tuple-element.25) | copy-start | bytes 786436
  122.9 6.9 %copy-start.4 = (f32[512,128]{1,0:T(8,128)S(1)}, f32[512,128]{1,0:T(8,128)}, u32[]{:S(2)}) copy-start(f32[512,128]{1,0:T(8,128)} %get-tuple-element.23) | copy-start | bytes 786436
  123.0 16.4 %collective-permute-start.3 = (f32[2,64,8]{2,1,0:T(8,128)S(1)}, f32[2,64,8]{2,1,0:T(8,128)S(1)}, u32[]{:S(2)}, u32[]{:S(2)}) collective-permute-start(f32[2,64,8]{2,1,0:T(8,128)S(1)} %pad_maximum_fusion), channel_id=1, source_target_pairs={{0,3},{1,2},{2,1},{3,0},{4,7},{5,6},{6,5},{7,4},{8,11},{9,10},{10,... | collective-permute-start | bytes 12296 | tf_op jit(solution)/shard_map/ppermute | solution.py:148
  129.7 7.7 %copy-start.9 = (f32[4,1,512]{2,1,0:T(1,128)S(1)}, f32[4,1,512]{2,1,0:T(1,128)}, u32[]{:S(2)}) copy-start(f32[4,1,512]{2,1,0:T(1,128)} %get-tuple-element.34) | copy-start | bytes 24580
  129.8 7.6 %copy-start.10 = (f32[4,1,512]{2,1,0:T(1,128)S(1)}, f32[4,1,512]{2,1,0:T(1,128)}, u32[]{:S(2)}) copy-start(f32[4,1,512]{2,1,0:T(1,128)} %get-tuple-element.35) | copy-start | bytes 24580
  129.8 8.4 %copy-start.3 = (f32[512,128]{1,0:T(8,128)S(1)}, f32[512,128]{1,0:T(8,128)}, u32[]{:S(2)}) copy-start(f32[512,128]{1,0:T(8,128)} %get-tuple-element.21) | copy-start | bytes 786436
  130.9 15.7 %copy-start.8 = (f32[4,1,512]{2,1,0:T(1,128)S(1)}, f32[4,1,512]{2,1,0:T(1,128)}, u32[]{:S(2)}) copy-start(f32[4,1,512]{2,1,0:T(1,128)} %get-tuple-element.36) | copy-start | bytes 24580
  130.9 26.5 %copy-start.11 = (f32[4,1,512]{2,1,0:T(1,128)S(1)}, f32[4,1,512]{2,1,0:T(1,128)}, u32[]{:S(2)}) copy-start(f32[4,1,512]{2,1,0:T(1,128)} %get-tuple-element.31) | copy-start | bytes 24580
  130.9 26.5 %copy-start.12 = (f32[4,1,512]{2,1,0:T(1,128)S(1)}, f32[4,1,512]{2,1,0:T(1,128)}, u32[]{:S(2)}) copy-start(f32[4,1,512]{2,1,0:T(1,128)} %get-tuple-element.29) | copy-start | bytes 24580
  131.0 26.5 %copy-start.13 = (f32[4,1,512]{2,1,0:T(1,128)S(1)}, f32[4,1,512]{2,1,0:T(1,128)}, u32[]{:S(2)}) copy-start(f32[4,1,512]{2,1,0:T(1,128)} %get-tuple-element.32) | copy-start | bytes 24580
  131.0 26.5 %copy-start.14 = (f32[4,1,512]{2,1,0:T(1,128)S(1)}, f32[4,1,512]{2,1,0:T(1,128)}, u32[]{:S(2)}) copy-start(f32[4,1,512]{2,1,0:T(1,128)} %get-tuple-element.30) | copy-start | bytes 24580
  140.1 16.6 %all-to-all-start.2 = ((f32[2,64,8]{2,0,1:T(2,128)}), f32[2,64,8]{2,0,1:T(2,128)S(1)}, u32[]{:S(2)}, u32[]{:S(2)}) async-start(f32[2,64,8]{2,0,1:T(2,128)} %copy.41), calls=%async_computation.2 | async-start | bytes 131072 | tf_op jit(solution)/shard_map/all_to_all | solution.py:150
  146.6 10.8 %collective-permute-start.4 = (f32[4,512]{1,0:T(4,128)S(1)}, f32[4,512]{1,0:T(4,128)S(1)}, u32[]{:S(2)}, u32[]{:S(2)}) collective-permute-start(f32[4,512]{1,0:T(4,128)S(1)} %bitcast.97), channel_id=1, source_target_pairs={{0,1},{1,0},{2,3},{3,2},{4,5},{5,4},{6,7},{7,6},{8,9},{9,8},{10,11... | collective-permute-start | bytes 24584 | tf_op jit(solution)/shard_map/ppermute | solution.py:145
  (1 other events, 1.3 us)

commit v4 on v2

--- a/solution.py
+++ b/solution.py
@@ -1,8 +1,6 @@
 import jax
 import jax.numpy as jnp
 from jax import lax
-from jax.experimental import pallas as pl
-from jax.experimental.pallas import tpu as pltpu
 from jax.sharding import PartitionSpec as P
 
 SLICE = 8
@@ -18,60 +16,16 @@
     )
 
 
-def _score_kernel(rowmask_ref, colvalid_ref, lhs_ref, rhs_ref, rowmax_ref, colmax_ref):
-    step = pl.program_id(0)
-    scores = lax.dot_general(
-        lhs_ref[...], rhs_ref[...], (((1,), (1,)), ((), ())), preferred_element_type=jnp.float32
-    )
-    keep = (rowmask_ref[0] > 0) & (colvalid_ref[0] > 0)
-    scores = jnp.where(keep, scores, jnp.float32(-1.0))
-    row_best = jnp.max(scores, axis=1, keepdims=True)
-    colmax_ref[0] = jnp.max(scores, axis=0, keepdims=True)
-
-    @pl.when(step == 0)
-    def _():
-        rowmax_ref[...] = jnp.broadcast_to(row_best, rowmax_ref.shape)
-
-    @pl.when(step > 0)
-    def _():
-        rowmax_ref[...] = jnp.maximum(rowmax_ref[...], row_best)
-
-
-def lent_scores(lent, row_valid, listed, columns, col_valid):
+def lent_scores(lent, row_valid, listed, columns, col_limit):
     slots, lent_rows, width = lent.shape
     owned, quarter, _ = columns.shape
-    n_rows = slots * lent_rows
-    tiles = owned
-    flat_rows = lent.reshape(n_rows, width)
-    flat_cols = columns.reshape(tiles * quarter, width)
-    rowmask = (row_valid[None, :, :] & jnp.transpose(listed)[:, :, None]).astype(jnp.int32)
-    rowmask = rowmask.reshape(owned, n_rows, 1)
-    colmask = col_valid.astype(jnp.int32).reshape(tiles, 1, quarter)
-    rowmax, colmax = pl.pallas_call(
-        _score_kernel,
-        out_shape=(
-            jax.ShapeDtypeStruct((n_rows, 128), jnp.float32),
-            jax.ShapeDtypeStruct((tiles, 1, quarter), jnp.float32),
-        ),
-        grid=(tiles,),
-        in_specs=[
-            pl.BlockSpec((1, n_rows, 1), lambda j: (j, 0, 0)),
-            pl.BlockSpec((1, 1, quarter), lambda j: (j, 0, 0)),
-            pl.BlockSpec((n_rows, width), lambda j: (0, 0)),
-            pl.BlockSpec((quarter, width), lambda j: (j, 0)),
-        ],
-        out_specs=[
-            pl.BlockSpec((n_rows, 128), lambda j: (0, 0)),
-            pl.BlockSpec((1, 1, quarter), lambda j: (j, 0, 0)),
-        ],
-        compiler_params=pltpu.CompilerParams(dimension_semantics=("arbitrary",)),
-        cost_estimate=pl.CostEstimate(
-            flops=2 * n_rows * tiles * quarter * width,
-            transcendentals=0,
-            bytes_accessed=2 * (n_rows + tiles * quarter) * width,
-        ),
-    )(rowmask, colmask, flat_rows, flat_cols)
-    return rowmax[:, 0].reshape(slots, lent_rows), colmax.reshape(owned, quarter)
+    flat_rows = lent.reshape(slots * lent_rows, width)
+    scores = jnp.einsum("rd,kcd->rkc", flat_rows, columns, preferred_element_type=jnp.float32)
+    scores = scores.reshape(slots, lent_rows, owned, quarter)
+    col_valid = jnp.arange(quarter, dtype=jnp.int32)[None, :] < col_limit[:, None]
+    keep = row_valid[:, :, None, None] & listed[:, None, :, None] & col_valid[None, None, :, :]
+    scores = jnp.where(keep, scores, jnp.float32(-1.0))
+    return jnp.max(scores, axis=(2, 3)), jnp.max(scores, axis=(0, 1))
 
 
 def on_device(embeds, fetch_list, partners, counts):
@@ -94,8 +48,8 @@
     positions = jnp.arange(quarter, dtype=jnp.int32)
     col_sources = []
     for lane, unit in ((my_lane, own_unit), (lane_p, other_unit)):
-        col_valid = (lane * quarter + positions)[None, :] < own_counts[:, None]
-        col_sources.append((unit, col_valid))
+        col_limit = (own_counts - lane * quarter).astype(jnp.int32)
+        col_sources.append((unit, col_limit))
     slice_offsets = jnp.arange(slice_rows, dtype=jnp.int32)
     local_ids = jnp.arange(owned, dtype=jnp.int32)
     piece_ids = jnp.arange(pieces, dtype=jnp.int32)
@@ -124,8 +78,8 @@
         ):
             row_valid = (lane * quarter + piece_rows) < arrived_counts[:, None]
             row_best = jnp.full(row_valid.shape, -1.0, jnp.float32)
-            for source, (unit, col_valid) in enumerate(col_sources):
-                rows_max, col_best = lent_scores(rows_in, row_valid, listed, unit, col_valid)
+            for source, (unit, col_limit) in enumerate(col_sources):
+                rows_max, col_best = lent_scores(rows_in, row_valid, listed, unit, col_limit)
                 row_best = jnp.maximum(row_best, rows_max)
                 col_part[source] = jnp.maximum(col_part[source], col_best)
             parts.append(row_best)

time: 154 us -> 151 us (0.981)
  Pallas kernels: 45.3 us -> 0 us
  matrix products: 0 us -> 37.7 us
  waiting for transfers between devices: 42.2 us -> 54 us
  other arithmetic: 15.1 us -> 9.51 us
  local copies, waits for them, and re-layouts: 14.9 us -> 11.5 us
  starting transfers between devices: 34.5 us -> 37.2 us
    pallas_call x8 -> x0, Pallas kernels: 45.3 us -> none  [lent_scores(): pl.pallas_call(_score_kernel, out_shape=(jax.ShapeDtypeStruct((n_rows, 12...]
    dot_general x0 -> x8, matrix products: none -> 37.7 us  [lent_scores(): jnp.einsum('rd,kcd->rkc', flat_rows, columns, preferred_element_type=jnp....]
    ppermute x2, waiting for transfers between devices: 0.01 us -> 9.45 us  [on_device(): arrived_other = lax.ppermute(arrived, 'gy', pair_r)]
    convert_element_type x3 -> x0, other arithmetic: 3.81 us -> none  [the longest x2 3.13 us: lent_scores(): (row_valid[None, :, :] & jnp.transpose(listed)[:, :, None]).astype(jnp.in...]
    all_to_all x2, waiting for transfers between devices: 30.3 us -> 32.7 us  [on_device(): lax.all_to_all(outbound, 'gx', split_axis=0, concat_axis=0, tiled=True)]
    ppermute x1, starting transfers between devices: 0.28 us -> 2.56 us  [on_device(): row_back = lax.ppermute(row_other, 'gy', pair_r)]
    unnamed x41 -> x6, local copies, waits for them, and re-layouts: 1.9 us -> 0.01 us
  transfers between devices with their start and end apart: 8 -> 8, of which waited for: 4 -> 5; matrix products, arithmetic and copies ran while one was open for 11% -> 22% of each run, Pallas kernels for 15% -> 0%
where the time goes in v4:
time: 151 us; the launch traced here: 150 us
  waiting for transfers between devices  54 us (36%)
  matrix products  37.7 us (25%)
  starting transfers between devices  37.2 us (25%)
  local copies, waits for them, and re-layouts  11.5 us (8%)
  other arithmetic  9.51 us (6%)
    dot_general x8, matrix products, lent_scores(): jnp.einsum('rd,kcd->rkc', flat_rows, columns, preferred_element_type=jnp....  37.7 us
    all_to_all x2, waiting for transfers between devices, on_device(): lax.all_to_all(outbound, 'gx', split_axis=0, concat_axis=0, tiled=True)  32.7 us
    all_to_all x2, starting transfers between devices, on_device(): lax.all_to_all(outbound, 'gx', split_axis=0, concat_axis=0, tiled=True)  19.3 us
    all_to_all x1, waiting for transfers between devices, on_device(): lax.all_to_all(row_mine, 'gx', split_axis=1, concat_axis=1, tiled=True)  9.97 us
    ppermute x2, waiting for transfers between devices, on_device(): arrived_other = lax.ppermute(arrived, 'gy', pair_r)  9.45 us
    all_to_all x1, starting transfers between devices, on_device(): lax.all_to_all(row_mine, 'gx', split_axis=1, concat_axis=1, tiled=True)  8.93 us
    gather x2, local copies, waits for them, and re-layouts, on_device(): outbound = own_pieces[outgoing_sent_block, outgoing_sent_piece]  7 us
    ppermute x2, starting transfers between devices, on_device(): arrived_other = lax.ppermute(arrived, 'gy', pair_r)  5.04 us
  transfers between devices with their start and end apart: 8, of which 5 were waited for; matrix products, arithmetic and copies ran while one was open for 22% of the time, Pallas kernels for 0%

profile of v4, /device:TPU:1, one launch (start us, length us, event | category | flops | bytes accessed | tf_op | source)
XLA Modules:
  0.0 150.2 jit_solution(18409847713368952280)
XLA Ops:
  0.9 2.6 %fusion = f32[4,512]{1,0:T(4,128)S(1)} fusion(bf16[4,512,768]{2,1,0:T(8,128)(2,1)} %param.4), kind=kLoop, calls=%fused_computation.6 | loop fusion | flops 4716544 | bytes 3153920 | tf_op jit(solution)/shard_map/reduce_sum | solution.py:14
  3.6 2.3 %fusion.71 = bf16[4,64,8,768]{3,2,1,0:T(8,128)(2,1)} fusion(f32[4,512]{1,0:T(4,128)S(1)} %add_rsqrt_fusion, bf16[4,512,768]{2,1,0:T(8,128)(2,1)S(1)} %copy-done.1), kind=kLoop, calls=%fused_computation.172 | loop fusion | flops 4718592 | bytes 6299648 | tf_op jit(solution)/shard_map/reshape | solution.py:46
  6.1 3.5 %gather_fusion.3 = bf16[64,8,768]{2,1,0:T(8,128)(2,1)} fusion(bf16[4,64,8,768]{3,2,1,0:T(8,128)(2,1)} %fusion.71, s32[64]{0:T(128)S(1)} %fusion.64), kind=kCustom, calls=%fused_computation.3 | custom fusion | bytes 1573376 | tf_op jit(solution)/shard_map/gather | solution.py:67
  9.6 13.4 %all-to-all-start.1 = ((bf16[64,8,768]{2,1,0:T(8,128)(2,1)}), bf16[64,8,768]{2,1,0:T(8,128)(2,1)}, u32[]{:S(2)}, u32[]{:S(2)}) async-start(bf16[64,8,768]{2,1,0:T(8,128)(2,1)} %gather_fusion.3), calls=%async_computation.1 | async-start | bytes 1572864 | tf_op jit(solution)/shard_map/all_to_all | solution.py:68
  23.0 2.2 %fusion.1 = bf16[4,512,768]{2,1,0:T(8,128)(2,1)} fusion(bf16[4,512,768]{2,1,0:T(8,128)(2,1)S(1)} %copy-done.1, f32[4,512]{1,0:T(4,128)S(1)} %add_rsqrt_fusion), kind=kLoop, calls=%fused_computation.7 | loop fusion | flops 4718592 | bytes 6299648 | tf_op jit(solution)/shard_map/convert_element_type | solution.py:14
  29.1 3.5 %gather_fusion.1 = bf16[64,8,768]{2,1,0:T(8,128)(2,1)} fusion(bf16[4,64,8,768]{3,2,1,0:T(8,128)(2,1)} %fusion.71, s32[64]{0:T(128)S(1)} %fusion.65), kind=kCustom, calls=%fused_computation.1 | custom fusion | bytes 1573376 | tf_op jit(solution)/shard_map/gather | solution.py:67
  32.9 13.1 %all-to-all-done.1 = bf16[64,8,768]{2,1,0:T(8,128)(2,1)} async-done(((bf16[64,8,768]{2,1,0:T(8,128)(2,1)}), bf16[64,8,768]{2,1,0:T(8,128)(2,1)}, u32[]{:S(2)}, u32[]{:S(2)}) %all-to-all-start.1) | async-done | bytes 786464 | tf_op jit(solution)/shard_map/all_to_all | solution.py:68
  46.0 5.9 %all-to-all-start = ((bf16[64,8,768]{2,1,0:T(8,128)(2,1)}), bf16[64,8,768]{2,1,0:T(8,128)(2,1)S(1)}, u32[]{:S(2)}, u32[]{:S(2)}) async-start(bf16[64,8,768]{2,1,0:T(8,128)(2,1)} %gather_fusion.1), calls=%async_computation | async-start | bytes 1572864 | tf_op jit(solution)/shard_map/all_to_all | solution.py:68
  52.7 2.6 %collective-permute-start.2 = (bf16[64,8,768]{2,1,0:T(8,128)(2,1)}, bf16[64,8,768]{2,1,0:T(8,128)(2,1)S(1)}, u32[]{:S(2)}, u32[]{:S(2)}) collective-permute-start(bf16[64,8,768]{2,1,0:T(8,128)(2,1)} %all-to-all-done.1), channel_id=1, source_target_pairs={{0,3},{1,2},{2,1},{3,0},{4,7},{5,6},{6,5},{7,4},{8,11},{9,10},{10,... | collective-permute-start | bytes 2359304 | tf_op jit(solution)/shard_map/ppermute | solution.py:69
  55.3 19.6 %all-to-all-done = bf16[64,8,768]{2,1,0:T(8,128)(2,1)S(1)} async-done(((bf16[64,8,768]{2,1,0:T(8,128)(2,1)}), bf16[64,8,768]{2,1,0:T(8,128)(2,1)S(1)}, u32[]{:S(2)}, u32[]{:S(2)}) %all-to-all-start) | async-done | bytes 786464 | tf_op jit(solution)/shard_map/all_to_all | solution.py:68
  74.9 2.5 %collective-permute-start.1 = (bf16[64,8,768]{2,1,0:T(8,128)(2,1)S(1)}, bf16[64,8,768]{2,1,0:T(8,128)(2,1)S(1)}, u32[]{:S(2)}, u32[]{:S(2)}) collective-permute-start(bf16[64,8,768]{2,1,0:T(8,128)(2,1)S(1)} %all-to-all-done), channel_id=1, source_target_pairs={{0,3},{1,2},{2,1},{3,0},{4,7},{5,6},{6,5},{7,4},{8,11},{9,10},{10,... | collective-permute-start | bytes 2359304 | tf_op jit(solution)/shard_map/ppermute | solution.py:69
  77.4 4.0 %fusion.30 = f32[64,8,4,512]{3,1,2,0:T(8,128)S(1)} fusion(bf16[4,512,768]{2,1,0:T(8,128)(2,1)} %fusion.1, bf16[64,8,768]{2,1,0:T(8,128)(2,1)} %all-to-all-done.1), kind=kOutput, calls=%fused_computation.44 | convolution fusion | flops 1610612736 | bytes 8126464 | tf_op jit(solution)/shard_map/rd,kcd->rkc/dot_general | solution.py:23
  81.3 3.7 %fusion.32 = f32[64,8,4,512]{3,1,2,0:T(8,128)S(1)} fusion(bf16[4,512,768]{2,1,0:T(8,128)(2,1)} %fusion.1, bf16[64,8,768]{2,1,0:T(8,128)(2,1)S(1)} %all-to-all-done), kind=kOutput, calls=%fused_computation.46 | convolution fusion | flops 1610612736 | bytes 8126464 | tf_op jit(solution)/shard_map/rd,kcd->rkc/dot_general | solution.py:23
  85.1 9.4 %collective-permute-done.1 = bf16[64,8,768]{2,1,0:T(8,128)(2,1)S(1)} collective-permute-done((bf16[64,8,768]{2,1,0:T(8,128)(2,1)S(1)}, bf16[64,8,768]{2,1,0:T(8,128)(2,1)S(1)}, u32[]{:S(2)}, u32[]{:S(2)}) %collective-permute-start.1) | collective-permute-done | bytes 786464 | tf_op jit(solution)/shard_map/ppermute | solution.py:69
  94.5 3.7 %fusion.28 = f32[64,8,4,512]{3,1,2,0:T(8,128)S(1)} fusion(bf16[4,512,768]{2,1,0:T(8,128)(2,1)} %fusion.1, bf16[64,8,768]{2,1,0:T(8,128)(2,1)S(1)} %collective-permute-done.1), kind=kOutput, calls=%fused_computation.42 | convolution fusion | flops 1610612736 | bytes 8126464 | tf_op jit(solution)/shard_map/rd,kcd->rkc/dot_general | solution.py:23
  98.2 3.7 %fusion.20 = f32[64,8,4,512]{3,1,2,0:T(8,128)S(1)} fusion(bf16[4,512,768]{2,1,0:T(8,128)(2,1)} %collective-permute-done, bf16[64,8,768]{2,1,0:T(8,128)(2,1)S(1)} %collective-permute-done.1), kind=kOutput, calls=%fused_computation.34 | convolution fusion | flops 1610612736 | bytes 8126464 | tf_op jit(solution)/shard_map/rd,kcd->rkc/dot_general | solution.py:23
  101.9 4.0 %fusion.22 = f32[64,8,4,512]{3,1,2,0:T(8,128)S(1)} fusion(bf16[4,512,768]{2,1,0:T(8,128)(2,1)} %collective-permute-done, bf16[64,8,768]{2,1,0:T(8,128)(2,1)} %all-to-all-done.1), kind=kOutput, calls=%fused_computation.36 | convolution fusion | flops 1610612736 | bytes 8126464 | tf_op jit(solution)/shard_map/rd,kcd->rkc/dot_general | solution.py:23
  105.9 3.7 %fusion.24 = f32[64,8,4,512]{3,1,2,0:T(8,128)S(1)} fusion(bf16[4,512,768]{2,1,0:T(8,128)(2,1)} %collective-permute-done, bf16[64,8,768]{2,1,0:T(8,128)(2,1)S(1)} %all-to-all-done), kind=kOutput, calls=%fused_computation.38 | convolution fusion | flops 1610612736 | bytes 8126464 | tf_op jit(solution)/shard_map/rd,kcd->rkc/dot_general | solution.py:23
  109.7 5.8 %fusion.18 = f32[64,8,4,512]{3,1,2,0:T(8,128)} fusion(bf16[4,512,768]{2,1,0:T(8,128)(2,1)} %collective-permute-done, bf16[64,8,768]{2,1,0:T(8,128)(2,1)S(1)} %collective-permute-done.2), kind=kOutput, calls=%fused_computation.32 | convolution fusion | flops 1610612736 | bytes 8126464 | tf_op jit(solution)/shard_map/rd,kcd->rkc/dot_general | solution.py:23
  115.4 9.2 %fusion.14 = (f32[4,512]{1,0:T(4,128)S(1)}, f32[64,8]{1,0:T(8,128)S(1)}, f32[64,8]{1,0:T(8,128)S(1)}, f32[4,512]{1,0:T(4,128)S(1)}, f32[4,512]{1,0:T(4,128)S(1)}...) fusion(pred[64,8,4]{1,2,0:T(4,128)(4,1)S(1)} %get-tuple-element, ...), kind=kOutput, calls=%fused_computation.28 | convolution fusion | flops 1644146688 | bytes 33386496 | tf_op jit(solution)/shard_map/rd,kcd->rkc/dot_general | solution.py:23
  124.6 2.6 %collective-permute-start.3 = (f32[2,64,8]{2,1,0:T(8,128)S(1)}, f32[2,64,8]{2,1,0:T(8,128)S(1)}, u32[]{:S(2)}, u32[]{:S(2)}) collective-permute-start(f32[2,64,8]{2,1,0:T(8,128)S(1)} %pad_maximum_fusion), channel_id=1, source_target_pairs={{0,3},{1,2},{2,1},{3,0},{4,7},{5,6},{6,5},{7,4},{8,11},{9,10},{10,... | collective-permute-start | bytes 12296 | tf_op jit(solution)/shard_map/ppermute | solution.py:89
  127.2 1.8 %collective-permute-done.3 = f32[2,64,8]{2,1,0:T(8,128)S(1)} collective-permute-done((f32[2,64,8]{2,1,0:T(8,128)S(1)}, f32[2,64,8]{2,1,0:T(8,128)S(1)}, u32[]{:S(2)}, u32[]{:S(2)}) %collective-permute-start.3) | collective-permute-done | bytes 4128 | tf_op jit(solution)/shard_map/ppermute | solution.py:89
  129.7 8.9 %all-to-all-start.2 = ((f32[2,64,8]{2,0,1:T(2,128)}), f32[2,64,8]{2,0,1:T(2,128)S(1)}, u32[]{:S(2)}, u32[]{:S(2)}) async-start(f32[2,64,8]{2,0,1:T(2,128)} %copy.31), calls=%async_computation.2 | async-start | bytes 131072 | tf_op jit(solution)/shard_map/all_to_all | solution.py:91
  138.8 10.0 %all-to-all-done.2 = f32[2,64,8]{2,0,1:T(2,128)S(1)} async-done(((f32[2,64,8]{2,0,1:T(2,128)}), f32[2,64,8]{2,0,1:T(2,128)S(1)}, u32[]{:S(2)}, u32[]{:S(2)}) %all-to-all-start.2) | async-done | bytes 4128 | tf_op jit(solution)/shard_map/all_to_all | solution.py:91
  (63 shorter events, 8.1 us)
Async XLA Ops:
  0.0 3.6 %copy-start.1 = (bf16[4,512,768]{2,1,0:T(8,128)(2,1)S(1)}, bf16[4,512,768]{2,1,0:T(8,128)(2,1)}, u32[]{:S(2)}) copy-start(bf16[4,512,768]{2,1,0:T(8,128)(2,1)} %param.4) | copy-start | bytes 9437188
  9.6 17.0 %copy-start = (s32[256]{0:T(256)S(1)}, s32[256]{0:T(256)}, u32[]{:S(2)}) copy-start(s32[256]{0:T(256)} %param.7) | copy-start | bytes 3076
  9.6 18.0 %copy-start.2 = (s32[2,64,64,2]{2,3,1,0:T(2,128)S(1)}, s32[2,64,64,2]{2,3,1,0:T(2,128)}, u32[]{:S(2)}) copy-start(s32[2,64,64,2]{2,3,1,0:T(2,128)} %param.6) | copy-start | bytes 196612
  9.6 36.4 %all-to-all-start.1 = ((bf16[64,8,768]{2,1,0:T(8,128)(2,1)}), bf16[64,8,768]{2,1,0:T(8,128)(2,1)}, u32[]{:S(2)}, u32[]{:S(2)}) async-start(bf16[64,8,768]{2,1,0:T(8,128)(2,1)} %gather_fusion.3), calls=%async_computation.1 | async-start | bytes 1572864 | tf_op jit(solution)/shard_map/all_to_all | solution.py:68
  25.3 72.9 %collective-permute-start = (bf16[4,512,768]{2,1,0:T(8,128)(2,1)}, bf16[4,512,768]{2,1,0:T(8,128)(2,1)}, u32[]{:S(2)}, u32[]{:S(2)}) collective-permute-start(bf16[4,512,768]{2,1,0:T(8,128)(2,1)} %fusion.1), channel_id=1, source_target_pairs={{0,1},{1,0},{2,3},{3,2},{4,5},{5,4},{6,7},{7,6},{8,9},{9,8},{10,11... | collective-permute-start | bytes 9437192 | tf_op jit(solution)/shard_map/ppermute | solution.py:45
  46.0 28.9 %all-to-all-start = ((bf16[64,8,768]{2,1,0:T(8,128)(2,1)}), bf16[64,8,768]{2,1,0:T(8,128)(2,1)S(1)}, u32[]{:S(2)}, u32[]{:S(2)}) async-start(bf16[64,8,768]{2,1,0:T(8,128)(2,1)} %gather_fusion.1), calls=%async_computation | async-start | bytes 1572864 | tf_op jit(solution)/shard_map/all_to_all | solution.py:68
  52.7 57.0 %collective-permute-start.2 = (bf16[64,8,768]{2,1,0:T(8,128)(2,1)}, bf16[64,8,768]{2,1,0:T(8,128)(2,1)S(1)}, u32[]{:S(2)}, u32[]{:S(2)}) collective-permute-start(bf16[64,8,768]{2,1,0:T(8,128)(2,1)} %all-to-all-done.1), channel_id=1, source_target_pairs={{0,3},{1,2},{2,1},{3,0},{4,7},{5,6},{6,5},{7,4},{8,11},{9,10},{10,... | collective-permute-start | bytes 2359304 | tf_op jit(solution)/shard_map/ppermute | solution.py:69
  74.9 19.6 %collective-permute-start.1 = (bf16[64,8,768]{2,1,0:T(8,128)(2,1)S(1)}, bf16[64,8,768]{2,1,0:T(8,128)(2,1)S(1)}, u32[]{:S(2)}, u32[]{:S(2)}) collective-permute-start(bf16[64,8,768]{2,1,0:T(8,128)(2,1)S(1)} %all-to-all-done), channel_id=1, source_target_pairs={{0,3},{1,2},{2,1},{3,0},{4,7},{5,6},{6,5},{7,4},{8,11},{9,10},{10,... | collective-permute-start | bytes 2359304 | tf_op jit(solution)/shard_map/ppermute | solution.py:69
  124.6 4.4 %collective-permute-start.3 = (f32[2,64,8]{2,1,0:T(8,128)S(1)}, f32[2,64,8]{2,1,0:T(8,128)S(1)}, u32[]{:S(2)}, u32[]{:S(2)}) collective-permute-start(f32[2,64,8]{2,1,0:T(8,128)S(1)} %pad_maximum_fusion), channel_id=1, source_target_pairs={{0,3},{1,2},{2,1},{3,0},{4,7},{5,6},{6,5},{7,4},{8,11},{9,10},{10,... | collective-permute-start | bytes 12296 | tf_op jit(solution)/shard_map/ppermute | solution.py:89
  129.7 19.0 %all-to-all-start.2 = ((f32[2,64,8]{2,0,1:T(2,128)}), f32[2,64,8]{2,0,1:T(2,128)S(1)}, u32[]{:S(2)}, u32[]{:S(2)}) async-start(f32[2,64,8]{2,0,1:T(2,128)} %copy.31), calls=%async_computation.2 | async-start | bytes 131072 | tf_op jit(solution)/shard_map/all_to_all | solution.py:91
  138.7 10.8 %collective-permute-start.4 = (f32[4,512]{1,0:T(4,128)S(1)}, f32[4,512]{1,0:T(4,128)S(1)}, u32[]{:S(2)}, u32[]{:S(2)}) collective-permute-start(f32[4,512]{1,0:T(4,128)S(1)} %maximum_maximum_fusion.2), channel_id=1, source_target_pairs={{0,1},{1,0},{2,3},{3,2},{4,5},{5,4},{6,7},{7,6},{8,9},{9,8},{10,11... | collective-permute-start | bytes 24584 | tf_op jit(solution)/shard_map/ppermute | solution.py:86

commit v5 on v4

--- a/solution.py
+++ b/solution.py
@@ -2,6 +2,7 @@
 import jax.numpy as jnp
 from jax import lax
 from jax.sharding import PartitionSpec as P
+
 
 SLICE = 8
 
@@ -28,7 +29,7 @@
     return jnp.max(scores, axis=(2, 3)), jnp.max(scores, axis=(0, 1))
 
 
-def on_device(embeds, fetch_list, partners, counts):
+def device_body(embeds, fetch_list, partners, counts):
     owned, quarter, width = embeds.shape
     slice_rows = SLICE
     pieces = quarter // slice_rows
@@ -54,10 +55,9 @@
     local_ids = jnp.arange(owned, dtype=jnp.int32)
     piece_ids = jnp.arange(pieces, dtype=jnp.int32)
     col_part = [jnp.full((owned, quarter), -1.0, jnp.float32) for _ in col_sources]
-    row_mine_parts = []
-    row_other_parts = []
     sent_blocks = []
     sent_pieces = []
+    jobs = []
     for wave_index in range(waves):
         tiles = lax.dynamic_index_in_dim(fetch_list[wave_index], my_group, 1, False)
         outgoing_sent_block = tiles // pieces - first
@@ -72,17 +72,22 @@
         chosen = lax.dynamic_index_in_dim(partners[wave_index], my_group, 0, False) - first
         listed = jnp.any(chosen[:, :, None] == local_ids[None, None, :], axis=1)
         piece_rows = (incoming % pieces)[:, None] * slice_rows + slice_offsets[None, :]
-        for lane, rows_in, parts in (
-            (my_lane, arrived, row_mine_parts),
-            (lane_r, arrived_other, row_other_parts),
-        ):
+        for part, (lane, rows_in) in enumerate(((my_lane, arrived), (lane_r, arrived_other))):
             row_valid = (lane * quarter + piece_rows) < arrived_counts[:, None]
-            row_best = jnp.full(row_valid.shape, -1.0, jnp.float32)
-            for source, (unit, col_limit) in enumerate(col_sources):
-                rows_max, col_best = lent_scores(rows_in, row_valid, listed, unit, col_limit)
-                row_best = jnp.maximum(row_best, rows_max)
-                col_part[source] = jnp.maximum(col_part[source], col_best)
-            parts.append(row_best)
+            jobs.append((wave_index, part, rows_in, row_valid, listed))
+    row_best = {}
+    token = None
+    for source, (unit, col_limit) in enumerate(col_sources):
+        for wave_index, part, rows_in, row_valid, listed in jobs:
+            if token is not None:
+                token, rows_in, unit = lax.optimization_barrier((token, rows_in, unit))
+            rows_max, col_best = lent_scores(rows_in, row_valid, listed, unit, col_limit)
+            token = (rows_max, col_best)
+            key = (wave_index, part)
+            row_best[key] = rows_max if key not in row_best else jnp.maximum(row_best[key], rows_max)
+            col_part[source] = jnp.maximum(col_part[source], col_best)
+    row_mine_parts = [row_best[(wave_index, 0)] for wave_index in range(waves)]
+    row_other_parts = [row_best[(wave_index, 1)] for wave_index in range(waves)]
     col_back = lax.ppermute(col_part[1], "gy", pair_p)
     col_total = jnp.maximum(col_part[0], col_back)
     row_other = jnp.stack(row_other_parts, axis=0)
@@ -110,5 +115,5 @@
     in_specs = (P("gx", "gy", None), P(), P(), P())
     out_specs = P("gx", "gy")
     return jax.shard_map(
-        on_device, mesh=mesh, in_specs=in_specs, out_specs=out_specs, check_vma=False
+        device_body, mesh=mesh, in_specs=in_specs, out_specs=out_specs, check_vma=False
     )

time: 151 us -> 142 us (0.940)
  waiting for transfers between devices: 54 us -> 48.5 us
  matrix products: 37.7 us -> 35 us
    ppermute x5, waiting for transfers between devices: 11.3 us -> 5.89 us  [the longest x2 4.05 us: device_body(): arrived_other = lax.ppermute(arrived, 'gy', pair_r)]
    dot_general x8, matrix products: 37.7 us -> 35 us  [lent_scores(): jnp.einsum('rd,kcd->rkc', flat_rows, columns, preferred_element_type=jnp....]
  transfers between devices with their start and end apart: 8 -> 8, of which waited for: 5 -> 5; matrix products, arithmetic and copies ran while one was open for 22% -> 20% of each run, Pallas kernels for 0% -> 0%
where the time goes in v5:
time: 142 us; the launch traced here: 141 us
  waiting for transfers between devices  48.5 us (34%)
  starting transfers between devices  36.4 us (26%)
  matrix products  35 us (25%)
  local copies, waits for them, and re-layouts  11.5 us (8%)
  other arithmetic  9.61 us (7%)
    dot_general x8, matrix products, lent_scores(): jnp.einsum('rd,kcd->rkc', flat_rows, columns, preferred_element_type=jnp....  35 us
    all_to_all x2, waiting for transfers between devices, device_body(): lax.all_to_all(outbound, 'gx', split_axis=0, concat_axis=0, tiled=True)  32.6 us
    all_to_all x2, starting transfers between devices, device_body(): lax.all_to_all(outbound, 'gx', split_axis=0, concat_axis=0, tiled=True)  19.2 us
    all_to_all x1, waiting for transfers between devices, device_body(): lax.all_to_all(row_mine, 'gx', split_axis=1, concat_axis=1, tiled=True)  9.97 us
    all_to_all x1, starting transfers between devices, device_body(): lax.all_to_all(row_mine, 'gx', split_axis=1, concat_axis=1, tiled=True)  8.29 us
    gather x2, local copies, waits for them, and re-layouts, device_body(): outbound = own_pieces[outgoing_sent_block, outgoing_sent_piece]  7 us
    ppermute x2, starting transfers between devices, device_body(): arrived_other = lax.ppermute(arrived, 'gy', pair_r)  5.04 us
    ppermute x2, waiting for transfers between devices, device_body(): arrived_other = lax.ppermute(arrived, 'gy', pair_r)  4.05 us
  transfers between devices with their start and end apart: 8, of which 5 were waited for; matrix products, arithmetic and copies ran while one was open for 20% of the time, Pallas kernels for 0%

profile of v5, /device:TPU:1, one launch (start us, length us, event | category | flops | bytes accessed | tf_op | source)
XLA Modules:
  0.0 141.3 jit_solution(15633913604223390842)
XLA Ops:
  0.9 2.6 %fusion = f32[4,512]{1,0:T(4,128)S(1)} fusion(bf16[4,512,768]{2,1,0:T(8,128)(2,1)} %param.4), kind=kLoop, calls=%fused_computation.6 | loop fusion | flops 4716544 | bytes 3153920 | tf_op jit(solution)/shard_map/reduce_sum | solution.py:15
  3.6 2.3 %fusion.71 = bf16[4,64,8,768]{3,2,1,0:T(8,128)(2,1)} fusion(f32[4,512]{1,0:T(4,128)S(1)} %add_rsqrt_fusion, bf16[4,512,768]{2,1,0:T(8,128)(2,1)S(1)} %copy-done.1), kind=kLoop, calls=%fused_computation.172 | loop fusion | flops 4718592 | bytes 6299648 | tf_op jit(solution)/shard_map/reshape | solution.py:47
  6.1 3.5 %gather_fusion.1 = bf16[64,8,768]{2,1,0:T(8,128)(2,1)} fusion(bf16[4,64,8,768]{3,2,1,0:T(8,128)(2,1)} %fusion.71, s32[64]{0:T(128)S(1)} %fusion.65), kind=kCustom, calls=%fused_computation.1 | custom fusion | bytes 1573376 | tf_op jit(solution)/shard_map/gather | solution.py:67
  9.6 13.3 %all-to-all-start = ((bf16[64,8,768]{2,1,0:T(8,128)(2,1)}), bf16[64,8,768]{2,1,0:T(8,128)(2,1)}, u32[]{:S(2)}, u32[]{:S(2)}) async-start(bf16[64,8,768]{2,1,0:T(8,128)(2,1)} %gather_fusion.1), calls=%async_computation | async-start | bytes 1572864 | tf_op jit(solution)/shard_map/all_to_all | solution.py:68
  22.9 2.3 %fusion.1 = bf16[4,512,768]{2,1,0:T(8,128)(2,1)} fusion(bf16[4,512,768]{2,1,0:T(8,128)(2,1)S(1)} %copy-done.1, f32[4,512]{1,0:T(4,128)S(1)} %add_rsqrt_fusion), kind=kLoop, calls=%fused_computation.7 | loop fusion | flops 4718592 | bytes 6299648 | tf_op jit(solution)/shard_map/convert_element_type | solution.py:15
  27.9 3.5 %gather_fusion.3 = bf16[64,8,768]{2,1,0:T(8,128)(2,1)} fusion(bf16[4,64,8,768]{3,2,1,0:T(8,128)(2,1)} %fusion.71, s32[64]{0:T(128)S(1)} %fusion.64), kind=kCustom, calls=%fused_computation.3 | custom fusion | bytes 1573376 | tf_op jit(solution)/shard_map/gather | solution.py:67
  32.6 13.2 %all-to-all-done = bf16[64,8,768]{2,1,0:T(8,128)(2,1)} async-done(((bf16[64,8,768]{2,1,0:T(8,128)(2,1)}), bf16[64,8,768]{2,1,0:T(8,128)(2,1)}, u32[]{:S(2)}, u32[]{:S(2)}) %all-to-all-start) | async-done | bytes 786464 | tf_op jit(solution)/shard_map/all_to_all | solution.py:68
  45.8 5.9 %all-to-all-start.1 = ((bf16[64,8,768]{2,1,0:T(8,128)(2,1)}), bf16[64,8,768]{2,1,0:T(8,128)(2,1)S(1)}, u32[]{:S(2)}, u32[]{:S(2)}) async-start(bf16[64,8,768]{2,1,0:T(8,128)(2,1)} %gather_fusion.3), calls=%async_computation.1 | async-start | bytes 1572864 | tf_op jit(solution)/shard_map/all_to_all | solution.py:68
  52.3 2.6 %collective-permute-start = (bf16[64,8,768]{2,1,0:T(8,128)(2,1)}, bf16[64,8,768]{2,1,0:T(8,128)(2,1)S(1)}, u32[]{:S(2)}, u32[]{:S(2)}) collective-permute-start(bf16[64,8,768]{2,1,0:T(8,128)(2,1)} %all-to-all-done), channel_id=1, source_target_pairs={{0,3},{1,2},{2,1},{3,0},{4,7},{5,6},{6,5},{7,4},{8,11},{9,10},{10,... | collective-permute-start | bytes 2359304 | tf_op jit(solution)/shard_map/ppermute | solution.py:69
  55.4 19.4 %all-to-all-done.1 = bf16[64,8,768]{2,1,0:T(8,128)(2,1)S(1)} async-done(((bf16[64,8,768]{2,1,0:T(8,128)(2,1)}), bf16[64,8,768]{2,1,0:T(8,128)(2,1)S(1)}, u32[]{:S(2)}, u32[]{:S(2)}) %all-to-all-start.1) | async-done | bytes 786464 | tf_op jit(solution)/shard_map/all_to_all | solution.py:68
  74.7 2.5 %collective-permute-start.1 = (bf16[64,8,768]{2,1,0:T(8,128)(2,1)S(1)}, bf16[64,8,768]{2,1,0:T(8,128)(2,1)S(1)}, u32[]{:S(2)}, u32[]{:S(2)}) collective-permute-start(bf16[64,8,768]{2,1,0:T(8,128)(2,1)S(1)} %all-to-all-done.1), channel_id=1, source_target_pairs={{0,3},{1,2},{2,1},{3,0},{4,7},{5,6},{6,5},{7,4},{8,11},{9,10},{10,... | collective-permute-start | bytes 2359304 | tf_op jit(solution)/shard_map/ppermute | solution.py:69
  77.2 4.2 %fusion.2 = (f32[4,512]{1,0:T(4,128)S(1)}, f32[64,8]{1,0:T(8,128)S(1)}) fusion(pred[4,512]{1,0:T(4,128)(4,1)S(1)} %iota_compare_fusion.5, pred[64,8,4]{1,2,0:T(4,128)(4,1)S(1)} %get-tuple-element.60, bf16[4,512,768]{2,1,0:T(8,128)(2,1)} %fusion.1, bf16[64,8,768]{2,1,0:T(8,128)(2,1)} %all-to-all-done), kind=kOutput, calls=%fused_computation.16 | convolution fusion | flops 1614804480 | bytes 3946496 | tf_op jit(solution)/shard_map/rd,kcd->rkc/dot_general | solution.py:24
  81.4 4.5 %fusion.10 = (f32[4,512]{1,0:T(4,128)S(1)}, f32[64,8]{1,0:T(8,128)S(1)}) fusion(pred[64,8,4]{1,2,0:T(4,128)(4,1)S(1)} %get-tuple-element.59, pred[4,512]{1,0:T(4,128)(4,1)S(1)} %iota_compare_fusion.5, bf16[4,512,768]{2,1,0:T(8,128)(2,1)} %fusion.1, bf16[64,8,768]{2,1,0:T(8,128)(2,1)S(1)} %collective-permute-done), kind=kOutput, calls=%fused_computation.24 | convolution fusion | flops 1614804480 | bytes 3946496 | tf_op jit(solution)/shard_map/rd,kcd->rkc/dot_general | solution.py:24
  85.9 4.4 %fusion.8 = (f32[4,512]{1,0:T(4,128)S(1)}, f32[64,8]{1,0:T(8,128)S(1)}) fusion(pred[64,8,4]{1,2,0:T(4,128)(4,1)S(1)} %get-tuple-element.58, pred[4,512]{1,0:T(4,128)(4,1)S(1)} %iota_compare_fusion.5, bf16[4,512,768]{2,1,0:T(8,128)(2,1)} %fusion.1, bf16[64,8,768]{2,1,0:T(8,128)(2,1)S(1)} %all-to-all-done.1), kind=kOutput, calls=%fused_computation.22 | convolution fusion | flops 1614804480 | bytes 3946496 | tf_op jit(solution)/shard_map/rd,kcd->rkc/dot_general | solution.py:24
  90.3 4.1 %collective-permute-done.1 = bf16[64,8,768]{2,1,0:T(8,128)(2,1)S(1)} collective-permute-done((bf16[64,8,768]{2,1,0:T(8,128)(2,1)S(1)}, bf16[64,8,768]{2,1,0:T(8,128)(2,1)S(1)}, u32[]{:S(2)}, u32[]{:S(2)}) %collective-permute-start.1) | collective-permute-done | bytes 786464 | tf_op jit(solution)/shard_map/ppermute | solution.py:69
  94.4 4.4 %fusion.6 = (f32[4,512]{1,0:T(4,128)S(1)}, f32[64,8]{1,0:T(8,128)S(1)}) fusion(pred[64,8,4]{1,2,0:T(4,128)(4,1)S(1)} %get-tuple-element.57, pred[4,512]{1,0:T(4,128)(4,1)S(1)} %iota_compare_fusion.5, bf16[4,512,768]{2,1,0:T(8,128)(2,1)} %fusion.1, bf16[64,8,768]{2,1,0:T(8,128)(2,1)S(1)} %collective-permute-done.1), kind=kOutput, calls=%fused_computation.20 | convolution fusion | flops 1614804480 | bytes 3946496 | tf_op jit(solution)/shard_map/rd,kcd->rkc/dot_general | solution.py:24
  98.8 4.2 %fusion.4 = (f32[4,512]{1,0:T(4,128)S(1)}, f32[64,8]{1,0:T(8,128)S(1)}) fusion(pred[4,512]{1,0:T(4,128)(4,1)S(1)} %iota_compare_fusion.4, pred[64,8,4]{1,2,0:T(4,128)(4,1)S(1)} %get-tuple-element.60, bf16[4,512,768]{2,1,0:T(8,128)(2,1)} %collective-permute-done.2, bf16[64,8,768]{2,1,0:T(8,128)(2,1)} %all-to-all-done), kind=kOutput, calls=%fused_computation.18 | convolution fusion | flops 1614804480 | bytes 3946496 | tf_op jit(solution)/shard_map/rd,kcd->rkc/dot_general | solution.py:24
  103.0 4.5 %fusion.14 = (f32[4,512]{1,0:T(4,128)S(1)}, f32[64,8]{1,0:T(8,128)S(1)}) fusion(pred[64,8,4]{1,2,0:T(4,128)(4,1)S(1)} %get-tuple-element.59, pred[4,512]{1,0:T(4,128)(4,1)S(1)} %iota_compare_fusion.4, bf16[4,512,768]{2,1,0:T(8,128)(2,1)} %collective-permute-done.2, bf16[64,8,768]{2,1,0:T(8,128)(2,1)S(1)} %collective-permute-done), kind=kOutput, calls=%fused_computation.28 | convolution fusion | flops 1614804480 | bytes 3946496 | tf_op jit(solution)/shard_map/rd,kcd->rkc/dot_general | solution.py:24
  107.5 4.5 %fusion.12 = (f32[4,512]{1,0:T(4,128)S(1)}, f32[64,8]{1,0:T(8,128)S(1)}) fusion(pred[64,8,4]{1,2,0:T(4,128)(4,1)S(1)} %get-tuple-element.58, pred[4,512]{1,0:T(4,128)(4,1)S(1)} %iota_compare_fusion.4, bf16[4,512,768]{2,1,0:T(8,128)(2,1)} %collective-permute-done.2, bf16[64,8,768]{2,1,0:T(8,128)(2,1)S(1)} %all-to-all-done.1), kind=kOutput, calls=%fused_computation.26 | convolution fusion | flops 1614804480 | bytes 3946496 | tf_op jit(solution)/shard_map/rd,kcd->rkc/dot_general | solution.py:24
  111.9 4.4 %fusion.16 = (f32[4,512]{1,0:T(4,128)S(1)}, f32[64,8]{1,0:T(8,128)S(1)}) fusion(pred[64,8,4]{1,2,0:T(4,128)(4,1)S(1)} %get-tuple-element.57, pred[4,512]{1,0:T(4,128)(4,1)S(1)} %iota_compare_fusion.4, bf16[4,512,768]{2,1,0:T(8,128)(2,1)} %collective-permute-done.2, bf16[64,8,768]{2,1,0:T(8,128)(2,1)S(1)} %collective-permute-done.1), kind=kOutput, calls=%fused_computation.30 | convolution fusion | flops 1614804480 | bytes 3946496 | tf_op jit(solution)/shard_map/rd,kcd->rkc/dot_general | solution.py:24
  116.4 2.6 %collective-permute-start.3 = (f32[2,64,8]{2,1,0:T(8,128)S(1)}, f32[2,64,8]{2,1,0:T(8,128)S(1)}, u32[]{:S(2)}, u32[]{:S(2)}) collective-permute-start(f32[2,64,8]{2,1,0:T(8,128)S(1)} %pad_maximum_fusion), channel_id=1, source_target_pairs={{0,3},{1,2},{2,1},{3,0},{4,7},{5,6},{6,5},{7,4},{8,11},{9,10},{10,... | collective-permute-start | bytes 12296 | tf_op jit(solution)/shard_map/ppermute | solution.py:94
  119.0 1.8 %collective-permute-done.3 = f32[2,64,8]{2,1,0:T(8,128)S(1)} collective-permute-done((f32[2,64,8]{2,1,0:T(8,128)S(1)}, f32[2,64,8]{2,1,0:T(8,128)S(1)}, u32[]{:S(2)}, u32[]{:S(2)}) %collective-permute-start.3) | collective-permute-done | bytes 4128 | tf_op jit(solution)/shard_map/ppermute | solution.py:94
  121.5 8.3 %all-to-all-start.2 = ((f32[2,64,8]{2,0,1:T(2,128)}), f32[2,64,8]{2,0,1:T(2,128)S(1)}, u32[]{:S(2)}, u32[]{:S(2)}) async-start(f32[2,64,8]{2,0,1:T(2,128)} %copy.31), calls=%async_computation.2 | async-start | bytes 131072 | tf_op jit(solution)/shard_map/all_to_all | solution.py:96
  129.9 10.0 %all-to-all-done.2 = f32[2,64,8]{2,0,1:T(2,128)S(1)} async-done(((f32[2,64,8]{2,0,1:T(2,128)}), f32[2,64,8]{2,0,1:T(2,128)S(1)}, u32[]{:S(2)}, u32[]{:S(2)}) %all-to-all-start.2) | async-done | bytes 4128 | tf_op jit(solution)/shard_map/all_to_all | solution.py:96
  (64 shorter events, 8.2 us)
Async XLA Ops:
  0.0 3.6 %copy-start.1 = (bf16[4,512,768]{2,1,0:T(8,128)(2,1)S(1)}, bf16[4,512,768]{2,1,0:T(8,128)(2,1)}, u32[]{:S(2)}) copy-start(bf16[4,512,768]{2,1,0:T(8,128)(2,1)} %param.4) | copy-start | bytes 9437188
  9.6 36.3 %all-to-all-start = ((bf16[64,8,768]{2,1,0:T(8,128)(2,1)}), bf16[64,8,768]{2,1,0:T(8,128)(2,1)}, u32[]{:S(2)}, u32[]{:S(2)}) async-start(bf16[64,8,768]{2,1,0:T(8,128)(2,1)} %gather_fusion.1), calls=%async_computation | async-start | bytes 1572864 | tf_op jit(solution)/shard_map/all_to_all | solution.py:68
  22.9 3.8 %copy-start = (s32[256]{0:T(256)S(1)}, s32[256]{0:T(256)}, u32[]{:S(2)}) copy-start(s32[256]{0:T(256)} %param.7) | copy-start | bytes 3076
  22.9 4.8 %copy-start.2 = (s32[2,64,64,2]{2,3,1,0:T(2,128)S(1)}, s32[2,64,64,2]{2,3,1,0:T(2,128)}, u32[]{:S(2)}) copy-start(s32[2,64,64,2]{2,3,1,0:T(2,128)} %param.6) | copy-start | bytes 196612
  25.2 73.6 %collective-permute-start.2 = (bf16[4,512,768]{2,1,0:T(8,128)(2,1)}, bf16[4,512,768]{2,1,0:T(8,128)(2,1)}, u32[]{:S(2)}, u32[]{:S(2)}) collective-permute-start(bf16[4,512,768]{2,1,0:T(8,128)(2,1)} %fusion.1), channel_id=1, source_target_pairs={{0,1},{1,0},{2,3},{3,2},{4,5},{5,4},{6,7},{7,6},{8,9},{9,8},{10,11... | collective-permute-start | bytes 9437192 | tf_op jit(solution)/shard_map/ppermute | solution.py:46
  45.8 28.9 %all-to-all-start.1 = ((bf16[64,8,768]{2,1,0:T(8,128)(2,1)}), bf16[64,8,768]{2,1,0:T(8,128)(2,1)S(1)}, u32[]{:S(2)}, u32[]{:S(2)}) async-start(bf16[64,8,768]{2,1,0:T(8,128)(2,1)} %gather_fusion.3), calls=%async_computation.1 | async-start | bytes 1572864 | tf_op jit(solution)/shard_map/all_to_all | solution.py:68
  52.3 29.1 %collective-permute-start = (bf16[64,8,768]{2,1,0:T(8,128)(2,1)}, bf16[64,8,768]{2,1,0:T(8,128)(2,1)S(1)}, u32[]{:S(2)}, u32[]{:S(2)}) collective-permute-start(bf16[64,8,768]{2,1,0:T(8,128)(2,1)} %all-to-all-done), channel_id=1, source_target_pairs={{0,3},{1,2},{2,1},{3,0},{4,7},{5,6},{6,5},{7,4},{8,11},{9,10},{10,... | collective-permute-start | bytes 2359304 | tf_op jit(solution)/shard_map/ppermute | solution.py:69
  74.7 19.6 %collective-permute-start.1 = (bf16[64,8,768]{2,1,0:T(8,128)(2,1)S(1)}, bf16[64,8,768]{2,1,0:T(8,128)(2,1)S(1)}, u32[]{:S(2)}, u32[]{:S(2)}) collective-permute-start(bf16[64,8,768]{2,1,0:T(8,128)(2,1)S(1)} %all-to-all-done.1), channel_id=1, source_target_pairs={{0,3},{1,2},{2,1},{3,0},{4,7},{5,6},{6,5},{7,4},{8,11},{9,10},{10,... | collective-permute-start | bytes 2359304 | tf_op jit(solution)/shard_map/ppermute | solution.py:69
  116.4 4.4 %collective-permute-start.3 = (f32[2,64,8]{2,1,0:T(8,128)S(1)}, f32[2,64,8]{2,1,0:T(8,128)S(1)}, u32[]{:S(2)}, u32[]{:S(2)}) collective-permute-start(f32[2,64,8]{2,1,0:T(8,128)S(1)} %pad_maximum_fusion), channel_id=1, source_target_pairs={{0,3},{1,2},{2,1},{3,0},{4,7},{5,6},{6,5},{7,4},{8,11},{9,10},{10,... | collective-permute-start | bytes 12296 | tf_op jit(solution)/shard_map/ppermute | solution.py:94
  121.5 18.4 %all-to-all-start.2 = ((f32[2,64,8]{2,0,1:T(2,128)}), f32[2,64,8]{2,0,1:T(2,128)S(1)}, u32[]{:S(2)}, u32[]{:S(2)}) async-start(f32[2,64,8]{2,0,1:T(2,128)} %copy.31), calls=%async_computation.2 | async-start | bytes 131072 | tf_op jit(solution)/shard_map/all_to_all | solution.py:96
  129.8 10.8 %collective-permute-start.4 = (f32[4,512]{1,0:T(4,128)S(1)}, f32[4,512]{1,0:T(4,128)S(1)}, u32[]{:S(2)}, u32[]{:S(2)}) collective-permute-start(f32[4,512]{1,0:T(4,128)S(1)} %maximum_maximum_fusion.2), channel_id=1, source_target_pairs={{0,1},{1,0},{2,3},{3,2},{4,5},{5,4},{6,7},{7,6},{8,9},{9,8},{10,11... | collective-permute-start | bytes 24584 | tf_op jit(solution)/shard_map/ppermute | solution.py:91
